TPU v7x, 128 devices: a whole 4x4x4 slice. The times are simulated.
128 devices in a mesh: gx: 16 (over z, y_hi, core), gy: 8 (over y_lo, x).
Axes of the slice: x: 4, y: 4 (y_hi: 2, y_lo: 2; y = y_hi * 2 + y_lo), z: 4, core: 2. Of those that a mesh axis runs over, the one named last changes fastest.
Arguments:
- velocity: float32 [3, 128, 64, 256], P(None, 'gy', 'gx'), may hold values from -6 to 6
- point_velocity: float32 [3, 16384], P(None, ('gx', 'gy')), may hold values from -8 to 8
- point_coef: float32 [16384], P(('gx', 'gy')), may hold values from 0.05 to 0.5
- point_width: float32 [16384], P(('gx', 'gy')), may hold values from 0.8 to 2
- send_point: int32 [128, 2048], P(('gx', 'gy')), may hold values from 0 to 127
- send_count: int32 [128, 128], P(('gx', 'gy')), may hold values from 0 to 16, as said below
- slot_offset: float32 [3, 128, 2048], P(None, ('gx', 'gy')), may hold values from 0.5 to 3.5
- send_anchor: int32 [128, 2048], P(('gx', 'gy')), may hold values from 0 to 12540, as said below
- vertical_inverse: float32 [64, 64], replicated, may hold values from -1 to 2, as said below
Outputs:
- new_velocity: float32 [3, 128, 64, 256], P(None, 'gy', 'gx')
Inputs may be any that keep to these rules, and one draw needn't show every extreme that they name: `send_count`: one destination tile, drawn from the seed, has 16 records from every source device. `send_anchor`: every block of 4 x 4 x 4 cells at the corner lies inside the destination tile: the corner is x * 4 * 256 + z * 256 + y with x <= 12, z <= 0, y <= 252. `vertical_inverse`: a dense matrix.
All inputs are finite; a program needn't handle non-finite values.
Results may differ from a plain program's by a relative error of at most 0.00007.
Values sent between devices are 32-bit elements; how exact they have to be, the bound alone decides.
No kernel may reach another device: no remote copies, remote signals or barrier semaphores. Data moves between devices by JAX's collectives and lax.ppermute only.
A program may use at most 64 MiB of HBM per device.

v0:
```python
import math

import jax
import jax.numpy as jnp
from jax import lax
from jax.sharding import PartitionSpec as P

K = 4


time_step = 0.25


def with_halo(block, sides, width, periodic):
    for axis, dim in sides:
        count = lax.axis_size(axis)
        forward = [(i, i + 1) for i in range(count - 1)]
        if periodic:
            forward.append((count - 1, 0))
        backward = [(target, source) for source, target in forward]
        low = lax.ppermute(
            lax.slice_in_dim(block, block.shape[dim] - width, None, axis=dim), axis, forward
        )
        high = lax.ppermute(lax.slice_in_dim(block, 0, width, axis=dim), axis, backward)
        block = jnp.concatenate([low, block, high], axis=dim)
    return block


def block_factor(corner, offset, extent, inverse_square, block_edge):
    cells = jnp.arange(extent, dtype=jnp.int32)[:, None]
    shifted = cells - corner[None, :]
    inside = (shifted >= 0) & (shifted < block_edge)
    spread = shifted.astype(jnp.float32) + 0.5 - offset[None, :]
    return jnp.where(inside, jnp.exp(-(spread * spread) * inverse_square[None, :]), 0.0)


def deposit_blocks(arrived, corner_x, corner_z, corner_y, rows_x, rows_z, rows_y, block_edge):
    width = arrived[6]
    inverse_square = 1.0 / (width * width)
    scaled = arrived[0:3] / (math.pi**1.5 * width**3)[None, :]
    along_x = block_factor(corner_x, arrived[3], rows_x, inverse_square, block_edge)
    along_z = block_factor(corner_z, arrived[4], rows_z, inverse_square, block_edge)
    along_y = block_factor(corner_y, arrived[5], rows_y, inverse_square, block_edge)
    left = scaled[:, None, None, :] * along_x[None, :, None, :] * along_z[None, None, :, :]
    left = left.reshape(3 * rows_x * rows_z, -1)
    result = lax.dot_general(
        left,
        along_y,
        (((1,), (1,)), ((), ())),
        precision=lax.Precision.HIGHEST,
        preferred_element_type=jnp.float32,
    )
    return result.reshape(3, rows_x, rows_z, rows_y)


def local(
    velocity,
    point_velocity,
    point_coef,
    point_width,
    send_point,
    send_count,
    slot_offset,
    send_anchor,
    vertical_inverse,
):
    rows_x = velocity.shape[1]
    rows_z = velocity.shape[2]
    rows_y = velocity.shape[3]
    slot_total = send_point.shape[1]
    device_count = lax.axis_size("gx") * lax.axis_size("gy")
    capacity = slot_total // device_count
    point_speed = jnp.sqrt(jnp.sum(point_velocity * point_velocity, axis=0))
    point_force = -(point_coef * point_speed)[None, :] * point_velocity
    chosen = send_point[0]
    limits = jnp.repeat(send_count[0], capacity)
    within = jnp.arange(slot_total, dtype=jnp.int32) % capacity < limits
    slot_force = jnp.take(point_force, chosen, axis=1) * within.astype(jnp.float32)[None, :]
    slot_width = jnp.take(point_width, chosen)[None, :]
    records = jnp.concatenate([slot_force, slot_offset[:, 0, :], slot_width], axis=0)
    arrived = lax.all_to_all(records, ("gx", "gy"), split_axis=1, concat_axis=1, tiled=True)
    anchors = send_anchor[0]
    corner_x = anchors // (rows_z * rows_y)
    remainder = anchors % (rows_z * rows_y)
    corner_z = remainder // rows_y
    corner_y = remainder % rows_y
    forcing = deposit_blocks(arrived, corner_x, corner_z, corner_y, rows_x, rows_z, rows_y, K)
    wide_x = with_halo(velocity, (("gy", 1),), 1, True)
    wide_z = with_halo(velocity, (("gx", 2),), 1, False)
    grad_x = (wide_x[:, 2:] - wide_x[:, :-2]) * 0.5
    grad_z = (wide_z[:, :, 2:] - wide_z[:, :, :-2]) * 0.5
    grad_y = (jnp.roll(velocity, -1, axis=3) - jnp.roll(velocity, 1, axis=3)) * 0.5
    transport = velocity[0:1] * grad_x + velocity[1:2] * grad_y + velocity[2:3] * grad_z
    updated = velocity + time_step * (forcing - transport)
    columns = lax.all_to_all(updated, "gx", split_axis=3, concat_axis=2, tiled=True)
    solved = jnp.einsum("zk,cxky->cxzy", vertical_inverse, columns, precision=lax.Precision.HIGHEST)
    new_velocity = lax.all_to_all(solved, "gx", split_axis=2, concat_axis=3, tiled=True)
    return new_velocity


def solution(mesh):
    placed = (
        P(None, "gy", "gx", None),
        P(None, ("gx", "gy")),
        P(("gx", "gy")),
        P(("gx", "gy")),
        P(("gx", "gy"), None),
        P(("gx", "gy"), None),
        P(None, ("gx", "gy"), None),
        P(("gx", "gy"), None),
        P(),
    )
    return jax.shard_map(
        local, mesh=mesh, in_specs=placed, out_specs=P(None, "gy", "gx", None), check_vma=False
    )
```

profile of v0, /device:TPU:1, one launch (start us, length us, event | category | flops | bytes accessed | tf_op | source)
XLA Modules:
  0.0 104.1 jit_solution(14867311447963179818)
XLA Ops:
  0.0 0.7 fusion.64
  0.8 2.1 %collective-permute-start.1 = (f32[3,1,4,256]{3,1,2,0:T(1,128)S(1)}, f32[3,1,4,256]{3,1,2,0:T(1,128)S(1)}, u32[]{:S(2)}, u32[]{:S(2)}) collective-permute-start(f32[3,1,4,256]{3,1,2,0:T(1,128)S(1)} %copy.145), channel_id=1, source_target_pairs={{0,1},{1,2},{2,3},{3,4},{4,5},{5,6},{6,7},{7,0},{8,9},{9,10},{10,1... | collective-permute-start | bytes 36872 | tf_op jit(solution)/shard_map/ppermute | solution.py:21
  2.9 2.4 %collective-permute-start = (f32[3,1,4,256]{3,1,2,0:T(1,128)S(1)}, f32[3,1,4,256]{3,1,2,0:T(1,128)S(1)}, u32[]{:S(2)}, u32[]{:S(2)}) collective-permute-start(f32[3,1,4,256]{3,1,2,0:T(1,128)S(1)} %copy.143), channel_id=1, source_target_pairs={{1,0},{2,1},{3,2},{4,3},{5,4},{6,5},{7,6},{0,7},{9,8},{10,9},{11,1... | collective-permute-start | bytes 36872 | tf_op jit(solution)/shard_map/ppermute | solution.py:24
  5.2 1.0 copy.158
  6.2 3.1 %collective-permute-start.2 = (f32[3,16,1,256]{3,1,2,0:T(8,128)S(1)}, f32[3,16,1,256]{3,1,2,0:T(8,128)S(1)}, u32[]{:S(2)}, u32[]{:S(2)}) collective-permute-start(f32[3,16,1,256]{3,1,2,0:T(8,128)S(1)} %get-tuple-element.22), channel_id=1, source_target_pairs={{8,0},{16,8},{24,16},{32,24},{40,32},{48,40},{56,48},{64,56},{72,6... | collective-permute-start | bytes 147464 | tf_op jit(solution)/shard_map/ppermute | solution.py:24
  9.3 4.8 %collective-permute-start.3 = (f32[3,16,1,256]{3,1,2,0:T(8,128)S(1)}, f32[3,16,1,256]{3,1,2,0:T(8,128)S(1)}, u32[]{:S(2)}, u32[]{:S(2)}) collective-permute-start(f32[3,16,1,256]{3,1,2,0:T(8,128)S(1)} %get-tuple-element.23), channel_id=1, source_target_pairs={{0,8},{8,16},{16,24},{24,32},{32,40},{40,48},{48,56},{56,64},{64,7... | collective-permute-start | bytes 147464 | tf_op jit(solution)/shard_map/ppermute | solution.py:21
  14.2 0.7 multiply_reduce_fusion
  14.9 0.7 multiply_negate_fusion
  15.5 0.7 broadcast_multiply_fusion.1
  16.2 0.7 compare_select_fusion.2
  17.4 1.4 %reduce.24 = s32[2048]{0:T(1024)S(1)} reduce(s32[1,2048]{1,0:T(1,128)} %param.13, s32[]{:T(128)} %broadcast.266), dimensions={0}, to_apply=%param.13.reduce_sub_computation.3 | reduce | bytes 16388 | tf_op args[4]
  18.9 12.6 %gather_fusion.1 = f32[2048]{0:T(1024)S(1)} fusion(f32[128]{0:T(128)S(1)} %copy-done.1, s32[2048]{0:T(1024)S(1)} %broadcast_clamp_fusion), kind=kCustom, calls=%fused_computation.1 | custom fusion | bytes 24576 | tf_op jit(solution)/shard_map/jit(_take)/gather | solution.py:79
  32.0 5.5 %gather_fusion = f32[2048,3]{1,0:T(8,128)S(1)} fusion(f32[3,128]{0,1:T(8,128)S(1)} %copy.139, s32[2048]{0:T(1024)S(1)} %broadcast_clamp_fusion), kind=kCustom, calls=%fused_computation | custom fusion | bytes 57344 | tf_op jit(solution)/shard_map/jit(_take)/gather | solution.py:78
  37.5 0.9 copy.140
  38.6 1.1 %copy.141 = f32[7,128,16]{2,0,1:T(8,128)} copy(f32[7,128,16]{2,1,0:T(8,128)S(1)} %pad_maximum_fusion) | data formatting | bytes 114688 | tf_op jit(solution)/shard_map/concatenate | solution.py:80
  39.7 7.9 %all-to-all-start = ((f32[7,128,16]{2,0,1:T(8,128)}), f32[7,128,16]{2,0,1:T(8,128)S(1)}, u32[]{:S(2)}, u32[]{:S(2)}) async-start(f32[7,128,16]{2,0,1:T(8,128)} %copy.141), calls=%async_computation | async-start | bytes 1048576 | tf_op jit(solution)/shard_map/all_to_all | solution.py:81
  48.1 13.5 %all-to-all-done = f32[7,128,16]{2,0,1:T(8,128)S(1)} async-done(((f32[7,128,16]{2,0,1:T(8,128)}), f32[7,128,16]{2,0,1:T(8,128)S(1)}, u32[]{:S(2)}, u32[]{:S(2)}) %all-to-all-start) | async-done | bytes 57376 | tf_op jit(solution)/shard_map/all_to_all | solution.py:81
  61.8 0.8 slice_reduce_fusion.2
  63.1 2.9 %fusion.35 = f32[3,16,4,256]{3,1,2,0:T(8,128)S(1)} fusion(f32[3,16,4,256]{3,1,2,0:T(8,128)S(1)} %copy.158, f32[3,16,1,256]{3,1,2,0:T(8,128)S(1)} %collective-permute-done.3, f32[3,16,1,256]{3,1,2,0:T(8,128)S(1)} %collective-permute-done.2, f32[3,1,4,256]{3,1,2,0:T(1,128)S(1)} %collective-permute-done.1, f32[3,1,4,256]{3,1,2,0:T(1,128)S(1)} %collective-permute-done, ...), kind=kOutput, calls=%fused_computation.36 | convolution fusion | flops 1214955520 | bytes 1556480 | tf_op jit(solution)/shard_map/dot_general | solution.py:46
  66.1 0.7 copy.159
  66.8 1.2 %reshape.289 = f32[16,1,3072]{2,1,0:T(1,128)S(1)} reshape(f32[256,3,4,16]{3,2,1,0:T(4,128)S(1)} %bitcast.44) | data formatting | bytes 393216
  68.0 11.6 %all_to_all.42 = f32[16,1,3072]{2,1,0:T(1,128)S(1)} all-to-all(f32[16,1,3072]{2,1,0:T(1,128)S(1)} %reshape.289), channel_id=1, replica_groups=mesh['gx'=16,'gy'=8] {'gx'}, dimensions={0} | all-to-all | bytes 393216 | tf_op jit(solution)/shard_map/all_to_all | solution.py:95
  80.2 1.1 %reduce.25 = f32[16,3072]{1,0:T(8,128)S(1)} reduce(f32[16,1,3072]{2,1,0:T(1,128)S(1)} %all_to_all.42, f32[]{:T(128)} %broadcast.267), dimensions={1}, to_apply=%all_to_all.31.reduce_sub_computation | reduce | bytes 393220 | tf_op jit(solution)/shard_map/all_to_all | solution.py:95
  81.3 1.1 %reshape.290 = f32[256,3,4,16]{3,2,1,0:T(4,128)S(1)} reshape(f32[16,3072]{1,0:T(8,128)S(1)} %reduce.25) | data formatting | bytes 393216
  82.4 0.7 copy.160
  83.1 3.5 %fusion.18 = f32[3,16,64,16]{2,3,1,0:T(8,128)} fusion(f32[3,16,64,16]{3,1,2,0:T(8,128)S(1)} %bitcast.46, f32[64,64]{1,0:T(8,128)S(1)} %copy-done), kind=kOutput, calls=%fused_computation.19 | convolution fusion | flops 37748736 | bytes 409600 | tf_op jit(solution)/shard_map/zk,cxky->cxzy/dot_general | solution.py:96
  86.5 1.7 %copy.162 = f32[3,16,64,16]{3,1,0,2:T(8,128)S(1)} copy(f32[3,16,64,16]{2,3,1,0:T(8,128)} %fusion.18) | data formatting | bytes 393216 | tf_op jit(solution)/shard_map/zk,cxky->cxzy/transpose | solution.py:96
  88.2 0.6 reshape.291
  88.8 11.4 %all_to_all.43 = f32[16,1,3072]{2,1,0:T(1,128)S(1)} all-to-all(f32[16,1,3072]{2,1,0:T(1,128)S(1)} %reshape.291), channel_id=1, replica_groups=mesh['gx'=16,'gy'=8] {'gx'}, dimensions={0} | all-to-all | bytes 393216 | tf_op jit(solution)/shard_map/all_to_all | solution.py:97
  100.2 1.1 %reduce.26 = f32[16,3072]{1,0:T(8,128)S(1)} reduce(f32[16,1,3072]{2,1,0:T(1,128)S(1)} %all_to_all.43, f32[]{:T(128)} %broadcast.267), dimensions={1}, to_apply=%all_to_all.35.reduce_sub_computation | reduce | bytes 393220 | tf_op jit(solution)/shard_map/all_to_all | solution.py:97
  101.9 0.9 copy.169
  102.8 1.3 %reshape.251 = f32[3,16,4,256]{3,2,1,0:T(4,128)} reshape(f32[3,16,4,16,16]{4,3,2,1,0:T(8,128)S(1)} %copy.169) | data formatting | bytes 393216 | tf_op jit(solution)/shard_map/all_to_all | solution.py:97
  (55 shorter events, 3.4 us)
Async XLA Ops:
  0.0 83.1 %copy-start = (f32[64,64]{1,0:T(8,128)S(1)}, f32[64,64]{1,0:T(8,128)}, u32[]{:S(2)}) copy-start(f32[64,64]{1,0:T(8,128)} %param.17) | copy-start | bytes 49156
  0.0 18.8 %copy-start.1 = (f32[128]{0:T(128)S(1)}, f32[128]{0:T(128)}, u32[]{:S(2)}) copy-start(f32[128]{0:T(128)} %param.12) | copy-start | bytes 1540
  0.8 62.3 %collective-permute-start.1 = (f32[3,1,4,256]{3,1,2,0:T(1,128)S(1)}, f32[3,1,4,256]{3,1,2,0:T(1,128)S(1)}, u32[]{:S(2)}, u32[]{:S(2)}) collective-permute-start(f32[3,1,4,256]{3,1,2,0:T(1,128)S(1)} %copy.145), channel_id=1, source_target_pairs={{0,1},{1,2},{2,3},{3,4},{4,5},{5,6},{6,7},{7,0},{8,9},{9,10},{10,1... | collective-permute-start | bytes 36872 | tf_op jit(solution)/shard_map/ppermute | solution.py:21
  2.9 60.2 %collective-permute-start = (f32[3,1,4,256]{3,1,2,0:T(1,128)S(1)}, f32[3,1,4,256]{3,1,2,0:T(1,128)S(1)}, u32[]{:S(2)}, u32[]{:S(2)}) collective-permute-start(f32[3,1,4,256]{3,1,2,0:T(1,128)S(1)} %copy.143), channel_id=1, source_target_pairs={{1,0},{2,1},{3,2},{4,3},{5,4},{6,5},{7,6},{0,7},{9,8},{10,9},{11,1... | collective-permute-start | bytes 36872 | tf_op jit(solution)/shard_map/ppermute | solution.py:24
  6.2 56.9 %collective-permute-start.2 = (f32[3,16,1,256]{3,1,2,0:T(8,128)S(1)}, f32[3,16,1,256]{3,1,2,0:T(8,128)S(1)}, u32[]{:S(2)}, u32[]{:S(2)}) collective-permute-start(f32[3,16,1,256]{3,1,2,0:T(8,128)S(1)} %get-tuple-element.22), channel_id=1, source_target_pairs={{8,0},{16,8},{24,16},{32,24},{40,32},{48,40},{56,48},{64,56},{72,6... | collective-permute-start | bytes 147464 | tf_op jit(solution)/shard_map/ppermute | solution.py:24
  9.3 53.8 %collective-permute-start.3 = (f32[3,16,1,256]{3,1,2,0:T(8,128)S(1)}, f32[3,16,1,256]{3,1,2,0:T(8,128)S(1)}, u32[]{:S(2)}, u32[]{:S(2)}) collective-permute-start(f32[3,16,1,256]{3,1,2,0:T(8,128)S(1)} %get-tuple-element.23), channel_id=1, source_target_pairs={{0,8},{8,16},{16,24},{24,32},{32,40},{40,48},{48,56},{56,64},{64,7... | collective-permute-start | bytes 147464 | tf_op jit(solution)/shard_map/ppermute | solution.py:21
  18.8 12.7 %copy-start.3 = (s32[1,2048]{1,0:T(1,128)S(1)}, s32[1,2048]{1,0:T(1,128)}, u32[]{:S(2)}) copy-start(s32[1,2048]{1,0:T(1,128)} %param.13) | copy-start | bytes 24580
  18.9 13.0 %copy-start.4 = (f32[3,1,2048]{2,1,0:T(1,128)S(1)}, f32[3,1,2048]{2,1,0:T(1,128)}, u32[]{:S(2)}) copy-start(f32[3,1,2048]{2,1,0:T(1,128)} %param.15) | copy-start | bytes 73732
  31.5 6.9 %copy-start.6 = (s32[1,128]{1,0:T(1,128)S(1)}, s32[1,128]{1,0:T(1,128)}, u32[]{:S(2)}) copy-start(s32[1,128]{1,0:T(1,128)} %param.14) | copy-start | bytes 1540
  38.6 9.2 %copy-start.5 = (s32[1,2048]{1,0:T(1,128)S(1)}, s32[1,2048]{1,0:T(1,128)}, u32[]{:S(2)}) copy-start(s32[1,2048]{1,0:T(1,128)} %param.16) | copy-start | bytes 24580
  38.6 9.4 %copy-start.2 = (f32[3,16,4,256]{3,2,1,0:T(4,128)S(1)}, f32[3,16,4,256]{3,2,1,0:T(4,128)}, u32[]{:S(2)}) copy-start(f32[3,16,4,256]{3,2,1,0:T(4,128)} %param.9) | copy-start | bytes 589828
  39.7 21.9 %all-to-all-start = ((f32[7,128,16]{2,0,1:T(8,128)}), f32[7,128,16]{2,0,1:T(8,128)S(1)}, u32[]{:S(2)}, u32[]{:S(2)}) async-start(f32[7,128,16]{2,0,1:T(8,128)} %copy.141), calls=%async_computation | async-start | bytes 1048576 | tf_op jit(solution)/shard_map/all_to_all | solution.py:81
where the time goes:
time: 105 us; the launch traced here: 104 us
  local copies, waits for them, and re-layouts  33.5 us (32%)
  blocking collectives  23 us (22%)
  starting transfers between devices  20.3 us (19%)
  waiting for transfers between devices  13.5 us (13%)
  other arithmetic  6.92 us (7%)
  matrix products  6.41 us (6%)
    all_to_all x1, waiting for transfers between devices, local(): lax.all_to_all(records, ('gx', 'gy'), split_axis=1, concat_axis=1, tiled=...  13.5 us
    gather x1, local copies, waits for them, and re-layouts, local(): slot_width = jnp.take(point_width, chosen)[None, :]  12.6 us
    all_to_all x1, blocking collectives, local(): lax.all_to_all(updated, 'gx', split_axis=3, concat_axis=2, tiled=True)  11.6 us
    all_to_all x1, blocking collectives, local(): lax.all_to_all(solved, 'gx', split_axis=2, concat_axis=3, tiled=True)  11.4 us
    all_to_all x1, starting transfers between devices, local(): lax.all_to_all(records, ('gx', 'gy'), split_axis=1, concat_axis=1, tiled=...  7.94 us
    ppermute x2, starting transfers between devices, with_halo(): lax.ppermute(lax.slice_in_dim(block, block.shape[dim] - width, None, axis...  6.93 us
    gather x2, local copies, waits for them, and re-layouts, local(): jnp.take(point_force, chosen, axis=1) * within.astype(jnp.float32)[None, :]  6.36 us
    ppermute x2, starting transfers between devices, with_halo(): lax.ppermute(lax.slice_in_dim(block, 0, width, axis=dim), axis, backward)  5.47 us
  transfers between devices with their start and end apart: 5, of which 1 were waited for; matrix products, arithmetic and copies ran while one was open for 27% of the time, Pallas kernels for 0%

commit v1 on v0

--- a/solution.py
+++ b/solution.py
@@ -75,8 +75,12 @@
     chosen = send_point[0]
     limits = jnp.repeat(send_count[0], capacity)
     within = jnp.arange(slot_total, dtype=jnp.int32) % capacity < limits
-    slot_force = jnp.take(point_force, chosen, axis=1) * within.astype(jnp.float32)[None, :]
-    slot_width = jnp.take(point_width, chosen)[None, :]
+    point_count = point_velocity.shape[1]
+    pick = (jnp.arange(point_count, dtype=jnp.int32)[:, None] == chosen[None, :]).astype(jnp.float32)
+    point_values = jnp.concatenate([point_force, point_width[None, :]], axis=0)
+    picked = jnp.dot(point_values, pick, precision=lax.Precision.HIGHEST, preferred_element_type=jnp.float32)
+    slot_force = picked[0:3] * within.astype(jnp.float32)[None, :]
+    slot_width = picked[3:4]
     records = jnp.concatenate([slot_force, slot_offset[:, 0, :], slot_width], axis=0)
     arrived = lax.all_to_all(records, ("gx", "gy"), split_axis=1, concat_axis=1, tiled=True)
     anchors = send_anchor[0]
@@ -92,9 +96,9 @@
     grad_y = (jnp.roll(velocity, -1, axis=3) - jnp.roll(velocity, 1, axis=3)) * 0.5
     transport = velocity[0:1] * grad_x + velocity[1:2] * grad_y + velocity[2:3] * grad_z
     updated = velocity + time_step * (forcing - transport)
-    columns = lax.all_to_all(updated, "gx", split_axis=3, concat_axis=2, tiled=True)
+    columns = lax.all_to_all(updated, "gx", split_axis=1, concat_axis=2, tiled=True)
     solved = jnp.einsum("zk,cxky->cxzy", vertical_inverse, columns, precision=lax.Precision.HIGHEST)
-    new_velocity = lax.all_to_all(solved, "gx", split_axis=2, concat_axis=3, tiled=True)
+    new_velocity = lax.all_to_all(solved, "gx", split_axis=2, concat_axis=1, tiled=True)
     return new_velocity
 
 

time: 105 us -> 64.9 us (0.62)
  local copies, waits for them, and re-layouts: 33.5 us -> 5.41 us
  waiting for transfers between devices: 13.5 us -> 2.28 us
  other arithmetic: 6.92 us -> 2.5 us
  blocking collectives: 23 us -> 27.3 us
  matrix products: 6.41 us -> 4.41 us
  starting transfers between devices: 20.3 us -> 22.2 us
    gather x3 -> x0, local copies, waits for them, and re-layouts: 19 us -> none  [the longest x1 12.6 us: local(): slot_width = jnp.take(point_width, chosen)[None, :]]
    all_to_all x1, waiting for transfers between devices: 13.5 us -> 2.27 us  [local(): lax.all_to_all(records, ('gx', 'gy'), split_axis=1, concat_axis=1, tiled=...]
    unnamed x20 -> x9, local copies, waits for them, and re-layouts: 4.9 us -> 0.45 us
    all_to_all x2, blocking collectives: 23 us -> 27.3 us  [the longest x1 15.9 us: local(): lax.all_to_all(updated, 'gx', split_axis=1, concat_axis=2, tiled=True)]
    all_to_all x1, starting transfers between devices: 7.94 us -> 11.5 us  [local(): lax.all_to_all(records, ('gx', 'gy'), split_axis=1, concat_axis=1, tiled=...]
    dot_general x1, matrix products: 3.46 us -> 0.32 us  [local(): jnp.einsum('zk,cxky->cxzy', vertical_inverse, columns, precision=lax.Prec...]
    ppermute x2, starting transfers between devices: 6.93 us -> 4.17 us  [with_halo(): lax.ppermute(lax.slice_in_dim(block, block.shape[dim] - width, None, axis...]
    all_to_all x4 -> x3, local copies, waits for them, and re-layouts: 3.44 us -> 0.76 us  [the longest x2 0.75 us: local(): lax.all_to_all(solved, 'gx', split_axis=2, concat_axis=1, tiled=True)]
  transfers between devices with their start and end apart: 5 -> 5, of which waited for: 1 -> 1; matrix products, arithmetic and copies ran while one was open for 27% -> 3% of each run, Pallas kernels for 0% -> 0%
where the time goes in v1:
time: 64.9 us; the launch traced here: 64.4 us
  blocking collectives  27.3 us (42%)
  starting transfers between devices  22.2 us (34%)
  local copies, waits for them, and re-layouts  5.41 us (8%)
  matrix products  4.41 us (7%)
  other arithmetic  2.5 us (4%)
  waiting for transfers between devices  2.28 us (4%)
    all_to_all x1, blocking collectives, local(): lax.all_to_all(updated, 'gx', split_axis=1, concat_axis=2, tiled=True)  15.9 us
    all_to_all x1, starting transfers between devices, local(): lax.all_to_all(records, ('gx', 'gy'), split_axis=1, concat_axis=1, tiled=...  11.5 us
    all_to_all x1, blocking collectives, local(): lax.all_to_all(solved, 'gx', split_axis=2, concat_axis=1, tiled=True)  11.4 us
    ppermute x2, starting transfers between devices, with_halo(): lax.ppermute(lax.slice_in_dim(block, 0, width, axis=dim), axis, backward)  6.51 us
    ppermute x2, starting transfers between devices, with_halo(): lax.ppermute(lax.slice_in_dim(block, block.shape[dim] - width, None, axis...  4.17 us
    dot_general x1, matrix products, deposit_blocks(): lax.dot_general(left, along_y, (((1,), (1,)), ((), ())), precision=lax.Pr...  2.95 us
    all_to_all x1, waiting for transfers between devices, local(): lax.all_to_all(records, ('gx', 'gy'), split_axis=1, concat_axis=1, tiled=...  2.27 us
    concatenate x4, local copies, waits for them, and re-layouts, local(): jnp.concatenate([slot_force, slot_offset[:, 0, :], slot_width], axis=0)  1.37 us
  transfers between devices with their start and end apart: 5, of which 1 were waited for; matrix products, arithmetic and copies ran while one was open for 3% of the time, Pallas kernels for 0%

profile of v1, /device:TPU:1, one launch (start us, length us, event | category | flops | bytes accessed | tf_op | source)
XLA Modules:
  0.0 64.4 jit_solution(6761563686099859529)
XLA Ops:
  0.0 0.7 %multiply_reduce_fusion = f32[128]{0:T(128)S(1)} fusion(f32[3,128]{1,0:T(4,128)} %param.10), kind=kLoop, calls=%fused_computation.89 | loop fusion | flops 640 | bytes 2048 | tf_op jit(solution)/shard_map/reduce_sum | solution.py:73
  0.7 0.7 %multiply_negate_fusion = f32[128]{0:T(128)S(1)} fusion(f32[128]{0:T(128)} %param.11, f32[128]{0:T(128)S(1)} %multiply_reduce_fusion), kind=kLoop, calls=%fused_computation.91 | loop fusion | flops 256 | bytes 1536 | tf_op jit(solution)/shard_map/neg | solution.py:74
  1.4 0.7 %broadcast_multiply_fusion.1 = f32[3,128]{1,0:T(4,128)S(1)} fusion(f32[3,128]{1,0:T(4,128)} %param.10, f32[128]{0:T(128)S(1)} %multiply_negate_fusion), kind=kLoop, calls=%fused_computation.90 | loop fusion | flops 384 | bytes 3584 | tf_op jit(solution)/shard_map/mul | solution.py:74
  2.1 0.7 %broadcast_in_dim.16 = s32[128,16]{1,0:T(8,128)S(1)} broadcast(s32[128]{0:T(128)} %bitcast.34), dimensions={0} | broadcast | bytes 8704 | tf_op jit(solution)/shard_map/broadcast_in_dim | solution.py:76
  2.8 0.1 reshape.201
  2.9 1.1 %fusion.23 = f32[4,2048]{1,0:T(4,128)S(1)} fusion(s32[2048]{0:T(1024)} %bitcast.35, f32[1,128]{1,0:T(1,128)} %bitcast.36, f32[3,128]{1,0:T(4,128)S(1)} %broadcast_multiply_fusion.1), kind=kOutput, calls=%fused_computation.24 | convolution fusion | flops 12845568 | bytes 43008 | tf_op jit(solution)/shard_map/dot_general | solution.py:81
  4.1 0.1 concatenate.36
  4.2 0.1 concatenate.38
  4.4 0.1 concatenate.37
  4.5 1.1 %copy.118 = f32[7,128,16]{2,0,1:T(8,128)} copy(f32[7,128,16]{2,1,0:T(8,128)S(1)} %pad_maximum_fusion) | data formatting | bytes 114688 | tf_op jit(solution)/shard_map/concatenate | solution.py:84
  5.6 11.5 %all-to-all-start = ((f32[7,128,16]{2,0,1:T(8,128)}), f32[7,128,16]{2,0,1:T(8,128)S(1)}, u32[]{:S(2)}, u32[]{:S(2)}) async-start(f32[7,128,16]{2,0,1:T(8,128)} %copy.118), calls=%async_computation | async-start | bytes 1048576 | tf_op jit(solution)/shard_map/all_to_all | solution.py:85
  17.2 3.0 %collective-permute-start.2 = (f32[3,16,1,256]{3,1,2,0:T(8,128)S(1)}, f32[3,16,1,256]{3,1,2,0:T(8,128)S(1)}, u32[]{:S(2)}, u32[]{:S(2)}) collective-permute-start(f32[3,16,1,256]{3,1,2,0:T(8,128)S(1)} %get-tuple-element.22), channel_id=1, source_target_pairs={{8,0},{16,8},{24,16},{32,24},{40,32},{48,40},{56,48},{64,56},{72,6... | collective-permute-start | bytes 147464 | tf_op jit(solution)/shard_map/ppermute | solution.py:24
  20.2 4.1 %collective-permute-start.3 = (f32[3,16,1,256]{3,1,2,0:T(8,128)S(1)}, f32[3,16,1,256]{3,1,2,0:T(8,128)S(1)}, u32[]{:S(2)}, u32[]{:S(2)}) collective-permute-start(f32[3,16,1,256]{3,1,2,0:T(8,128)S(1)} %get-tuple-element.23), channel_id=1, source_target_pairs={{0,8},{8,16},{16,24},{24,32},{32,40},{40,48},{48,56},{56,64},{64,7... | collective-permute-start | bytes 147464 | tf_op jit(solution)/shard_map/ppermute | solution.py:21
  24.3 3.5 %collective-permute-start = (f32[3,1,4,256]{3,1,2,0:T(1,128)S(1)}, f32[3,1,4,256]{3,1,2,0:T(1,128)S(1)}, u32[]{:S(2)}, u32[]{:S(2)}) collective-permute-start(f32[3,1,4,256]{3,1,2,0:T(1,128)S(1)} %copy.120), channel_id=1, source_target_pairs={{1,0},{2,1},{3,2},{4,3},{5,4},{6,5},{7,6},{0,7},{9,8},{10,9},{11,1... | collective-permute-start | bytes 36872 | tf_op jit(solution)/shard_map/ppermute | solution.py:24
  27.9 0.1 collective-permute-start.1
  27.9 0.1 fusion.63
  28.1 0.1 fusion.62
  28.2 0.4 copy-done.3
  28.8 2.3 %all-to-all-done = f32[7,128,16]{2,0,1:T(8,128)S(1)} async-done(((f32[7,128,16]{2,0,1:T(8,128)}), f32[7,128,16]{2,0,1:T(8,128)S(1)}, u32[]{:S(2)}, u32[]{:S(2)}) %all-to-all-start) | async-done | bytes 57376 | tf_op jit(solution)/shard_map/all_to_all | solution.py:85
  31.1 0.8 %slice_reduce_fusion.2 = (f32[128,16]{1,0:T(8,128)S(1)}, f32[128,16]{1,0:T(8,128)S(1)}, f32[128,16]{1,0:T(8,128)S(1)}, f32[128,16]{1,0:T(8,128)S(1)}) fusion(f32[7,128,16]{2,0,1:T(8,128)S(1)} %all-to-all-done), kind=kLoop, calls=%fused_computation.52 | loop fusion | bytes 65536 | tf_op jit(solution)/shard_map/slice | solution.py:41
  31.8 0.1 slice.88
  31.9 0.1 sub.116
  32.1 0.1 slice.86
  32.2 0.1 sub.123
  32.5 0.1 sub.130
  32.6 3.0 %fusion.32 = f32[3,16,4,256]{3,1,2,0:T(8,128)S(1)} fusion(f32[3,16,4,256]{3,1,2,0:T(8,128)S(1)} %copy.135, f32[3,16,1,256]{3,1,2,0:T(8,128)S(1)} %collective-permute-done.3, f32[3,16,1,256]{3,1,2,0:T(8,128)S(1)} %collective-permute-done.2, f32[3,1,4,256]{3,1,2,0:T(1,128)S(1)} %collective-permute-done.1, f32[3,1,4,256]{3,1,2,0:T(1,128)S(1)} %collective-permute-done, ...), kind=kOutput, calls=%fused_computation.35 | convolution fusion | flops 1214955520 | bytes 1556480 | tf_op jit(solution)/shard_map/dot_general | solution.py:46
  35.6 0.1 copy.136
  35.7 15.9 %all_to_all.27 = f32[3,16,4,256]{3,2,0,1:T(4,128)S(1)} all-to-all(f32[3,16,4,256]{3,2,0,1:T(4,128)S(1)} %copy.136), channel_id=1, replica_groups=mesh['gx'=16,'gy'=8] {'gx'}, dimensions={1} | all-to-all | bytes 393216 | tf_op jit(solution)/shard_map/all_to_all | solution.py:99
  51.8 0.3 convolution_bitcast_fusion
  52.1 0.2 copy.138
  52.3 11.4 %all_to_all.28 = f32[3,1,64,256]{3,1,0,2:T(1,128)S(1)} all-to-all(f32[3,1,64,256]{3,1,0,2:T(1,128)S(1)} %copy.138), channel_id=1, replica_groups=mesh['gx'=16,'gy'=8] {'gx'}, dimensions={2} | all-to-all | bytes 393216 | tf_op jit(solution)/shard_map/all_to_all | solution.py:101
  63.7 0.7 %all_to_all.23 = f32[3,16,4,256]{3,2,1,0:T(4,128)} reshape(f32[3,1,64,256]{3,2,0,1:T(8,128)S(1)} %copy.139) | data formatting | bytes 393216 | tf_op jit(solution)/shard_map/all_to_all | solution.py:101
  (38 shorter events, 0.8 us)
Async XLA Ops:
  0.0 51.8 %copy-start = (f32[64,64]{1,0:T(8,128)S(1)}, f32[64,64]{1,0:T(8,128)}, u32[]{:S(2)}) copy-start(f32[64,64]{1,0:T(8,128)} %param.17) | copy-start | bytes 49156
  0.0 4.3 %copy-start.2 = (f32[3,1,2048]{2,1,0:T(1,128)S(1)}, f32[3,1,2048]{2,1,0:T(1,128)}, u32[]{:S(2)}) copy-start(f32[3,1,2048]{2,1,0:T(1,128)} %param.15) | copy-start | bytes 73732
  5.6 11.5 %copy-start.1 = (f32[3,16,4,256]{3,2,1,0:T(4,128)S(1)}, f32[3,16,4,256]{3,2,1,0:T(4,128)}, u32[]{:S(2)}) copy-start(f32[3,16,4,256]{3,2,1,0:T(4,128)} %param.9) | copy-start | bytes 589828
  5.6 25.5 %all-to-all-start = ((f32[7,128,16]{2,0,1:T(8,128)}), f32[7,128,16]{2,0,1:T(8,128)S(1)}, u32[]{:S(2)}, u32[]{:S(2)}) async-start(f32[7,128,16]{2,0,1:T(8,128)} %copy.118), calls=%async_computation | async-start | bytes 1048576 | tf_op jit(solution)/shard_map/all_to_all | solution.py:85
  17.2 15.4 %collective-permute-start.2 = (f32[3,16,1,256]{3,1,2,0:T(8,128)S(1)}, f32[3,16,1,256]{3,1,2,0:T(8,128)S(1)}, u32[]{:S(2)}, u32[]{:S(2)}) collective-permute-start(f32[3,16,1,256]{3,1,2,0:T(8,128)S(1)} %get-tuple-element.22), channel_id=1, source_target_pairs={{8,0},{16,8},{24,16},{32,24},{40,32},{48,40},{56,48},{64,56},{72,6... | collective-permute-start | bytes 147464 | tf_op jit(solution)/shard_map/ppermute | solution.py:24
  20.2 12.5 %collective-permute-start.3 = (f32[3,16,1,256]{3,1,2,0:T(8,128)S(1)}, f32[3,16,1,256]{3,1,2,0:T(8,128)S(1)}, u32[]{:S(2)}, u32[]{:S(2)}) collective-permute-start(f32[3,16,1,256]{3,1,2,0:T(8,128)S(1)} %get-tuple-element.23), channel_id=1, source_target_pairs={{0,8},{8,16},{16,24},{24,32},{32,40},{40,48},{48,56},{56,64},{64,7... | collective-permute-start | bytes 147464 | tf_op jit(solution)/shard_map/ppermute | solution.py:21
  24.3 8.3 %collective-permute-start = (f32[3,1,4,256]{3,1,2,0:T(1,128)S(1)}, f32[3,1,4,256]{3,1,2,0:T(1,128)S(1)}, u32[]{:S(2)}, u32[]{:S(2)}) collective-permute-start(f32[3,1,4,256]{3,1,2,0:T(1,128)S(1)} %copy.120), channel_id=1, source_target_pairs={{1,0},{2,1},{3,2},{4,3},{5,4},{6,5},{7,6},{0,7},{9,8},{10,9},{11,1... | collective-permute-start | bytes 36872 | tf_op jit(solution)/shard_map/ppermute | solution.py:24
  27.8 0.7 %copy-start.3 = (s32[1,2048]{1,0:T(1,128)S(1)}, s32[1,2048]{1,0:T(1,128)}, u32[]{:S(2)}) copy-start(s32[1,2048]{1,0:T(1,128)} %param.16) | copy-start | bytes 24580
  27.9 4.7 %collective-permute-start.1 = (f32[3,1,4,256]{3,1,2,0:T(1,128)S(1)}, f32[3,1,4,256]{3,1,2,0:T(1,128)S(1)}, u32[]{:S(2)}, u32[]{:S(2)}) collective-permute-start(f32[3,1,4,256]{3,1,2,0:T(1,128)S(1)} %copy.122), channel_id=1, source_target_pairs={{0,1},{1,2},{2,3},{3,4},{4,5},{5,6},{6,7},{7,0},{8,9},{9,10},{10,1... | collective-permute-start | bytes 36872 | tf_op jit(solution)/shard_map/ppermute | solution.py:21

commit v2 on v1

--- a/solution.py
+++ b/solution.py
@@ -81,8 +81,14 @@
     picked = jnp.dot(point_values, pick, precision=lax.Precision.HIGHEST, preferred_element_type=jnp.float32)
     slot_force = picked[0:3] * within.astype(jnp.float32)[None, :]
     slot_width = picked[3:4]
-    records = jnp.concatenate([slot_force, slot_offset[:, 0, :], slot_width], axis=0)
-    arrived = lax.all_to_all(records, ("gx", "gy"), split_axis=1, concat_axis=1, tiled=True)
+    spare = jnp.zeros_like(slot_width)
+    records = jnp.concatenate([slot_force, slot_offset[:, 0, :], slot_width, spare], axis=0)
+    fields = records.shape[0]
+    records = records.reshape(fields, device_count, capacity).transpose(1, 0, 2)
+    records = records.reshape(device_count, fields * capacity)
+    arrived = lax.all_to_all(records, ("gx", "gy"), split_axis=0, concat_axis=0, tiled=True)
+    arrived = arrived.reshape(device_count, fields, capacity).transpose(1, 0, 2)
+    arrived = arrived.reshape(fields, slot_total)
     anchors = send_anchor[0]
     corner_x = anchors // (rows_z * rows_y)
     remainder = anchors % (rows_z * rows_y)

time: 64.9 us -> 62 us (0.955)
  starting transfers between devices: 22.2 us -> 20.7 us
  blocking collectives: 27.3 us -> 26.1 us
  waiting for transfers between devices: 2.28 us -> 1.63 us
    all_to_all x1, starting transfers between devices: 11.5 us -> 9.18 us  [local(): lax.all_to_all(records, ('gx', 'gy'), split_axis=0, concat_axis=0, tiled=...]
    ppermute x2, starting transfers between devices: 4.17 us -> 6.19 us  [with_halo(): lax.ppermute(lax.slice_in_dim(block, block.shape[dim] - width, None, axis...]
    all_to_all x1, blocking collectives: 15.9 us -> 14.7 us  [local(): lax.all_to_all(updated, 'gx', split_axis=1, concat_axis=2, tiled=True)]
    ppermute x2, starting transfers between devices: 6.51 us -> 5.34 us  [with_halo(): lax.ppermute(lax.slice_in_dim(block, 0, width, axis=dim), axis, backward)]
    all_to_all x0 -> x2, local copies, waits for them, and re-layouts: none -> 0.84 us  [local(): lax.all_to_all(records, ('gx', 'gy'), split_axis=0, concat_axis=0, tiled=...]
    concatenate x4 -> x7, local copies, waits for them, and re-layouts: 1.37 us -> 0.59 us  [local(): jnp.concatenate([slot_force, slot_offset[:, 0, :], slot_width, spare], ax...]
    slice x3, local copies, waits for them, and re-layouts: 0.03 us -> 0.76 us  [with_halo(): lax.slice_in_dim(block, 0, width, axis=dim)]
    slice x1 -> x2, local copies, waits for them, and re-layouts: 0.78 us -> 0.11 us  [deposit_blocks(): arrived[3]]
  transfers between devices with their start and end apart: 5 -> 5, of which waited for: 1 -> 1; matrix products, arithmetic and copies ran while one was open for 3% -> 11% of each run, Pallas kernels for 0% -> 0%
where the time goes in v2:
time: 62 us; the launch traced here: 61.5 us
  blocking collectives  26.1 us (42%)
  starting transfers between devices  20.7 us (33%)
  local copies, waits for them, and re-layouts  5.72 us (9%)
  matrix products  4.42 us (7%)
  other arithmetic  2.53 us (4%)
  waiting for transfers between devices  1.63 us (3%)
    all_to_all x1, blocking collectives, local(): lax.all_to_all(updated, 'gx', split_axis=1, concat_axis=2, tiled=True)  14.7 us
    all_to_all x1, blocking collectives, local(): lax.all_to_all(solved, 'gx', split_axis=2, concat_axis=1, tiled=True)  11.4 us
    all_to_all x1, starting transfers between devices, local(): lax.all_to_all(records, ('gx', 'gy'), split_axis=0, concat_axis=0, tiled=...  9.18 us
    ppermute x2, starting transfers between devices, with_halo(): lax.ppermute(lax.slice_in_dim(block, block.shape[dim] - width, None, axis...  6.19 us
    ppermute x2, starting transfers between devices, with_halo(): lax.ppermute(lax.slice_in_dim(block, 0, width, axis=dim), axis, backward)  5.34 us
    dot_general x1, matrix products, deposit_blocks(): lax.dot_general(left, along_y, (((1,), (1,)), ((), ())), precision=lax.Pr...  2.96 us
    all_to_all x1, waiting for transfers between devices, local(): lax.all_to_all(records, ('gx', 'gy'), split_axis=0, concat_axis=0, tiled=...  1.62 us
  transfers between devices with their start and end apart: 5, of which 1 were waited for; matrix products, arithmetic and copies ran while one was open for 11% of the time, Pallas kernels for 0%

profile of v2, /device:TPU:1, one launch (start us, length us, event | category | flops | bytes accessed | tf_op | source)
XLA Modules:
  0.0 61.5 jit_solution(956777573622410286)
XLA Ops:
  0.0 0.7 %fusion.64 = (f32[3,1,4,256]{3,2,1,0:T(4,128)S(1)}, f32[3,1,4,256]{3,2,1,0:T(4,128)S(1)}) fusion(f32[3,16,4,256]{3,2,1,0:T(4,128)} %param.9), kind=kLoop, calls=%fused_computation.95 | loop fusion | bytes 49152 | tf_op jit(solution)/shard_map/slice | solution.py:24
  0.8 2.1 %collective-permute-start.1 = (f32[3,1,4,256]{3,1,2,0:T(1,128)S(1)}, f32[3,1,4,256]{3,1,2,0:T(1,128)S(1)}, u32[]{:S(2)}, u32[]{:S(2)}) collective-permute-start(f32[3,1,4,256]{3,1,2,0:T(1,128)S(1)} %copy.121), channel_id=1, source_target_pairs={{0,1},{1,2},{2,3},{3,4},{4,5},{5,6},{6,7},{7,0},{8,9},{9,10},{10,1... | collective-permute-start | bytes 36872 | tf_op jit(solution)/shard_map/ppermute | solution.py:21
  2.9 2.4 %collective-permute-start = (f32[3,1,4,256]{3,1,2,0:T(1,128)S(1)}, f32[3,1,4,256]{3,1,2,0:T(1,128)S(1)}, u32[]{:S(2)}, u32[]{:S(2)}) collective-permute-start(f32[3,1,4,256]{3,1,2,0:T(1,128)S(1)} %copy.119), channel_id=1, source_target_pairs={{1,0},{2,1},{3,2},{4,3},{5,4},{6,5},{7,6},{0,7},{9,8},{10,9},{11,1... | collective-permute-start | bytes 36872 | tf_op jit(solution)/shard_map/ppermute | solution.py:24
  5.2 0.7 %multiply_reduce_fusion = f32[128]{0:T(128)S(1)} fusion(f32[3,128]{1,0:T(4,128)} %param.10), kind=kLoop, calls=%fused_computation.85 | loop fusion | flops 640 | bytes 2048 | tf_op jit(solution)/shard_map/reduce_sum | solution.py:73
  5.9 0.7 %multiply_negate_fusion = f32[128]{0:T(128)S(1)} fusion(f32[128]{0:T(128)} %param.11, f32[128]{0:T(128)S(1)} %multiply_reduce_fusion), kind=kLoop, calls=%fused_computation.87 | loop fusion | flops 256 | bytes 1536 | tf_op jit(solution)/shard_map/neg | solution.py:74
  6.6 0.7 %broadcast_multiply_fusion.1 = f32[3,128]{1,0:T(4,128)S(1)} fusion(f32[3,128]{1,0:T(4,128)} %param.10, f32[128]{0:T(128)S(1)} %multiply_negate_fusion), kind=kLoop, calls=%fused_computation.86 | loop fusion | flops 384 | bytes 3584 | tf_op jit(solution)/shard_map/mul | solution.py:74
  7.3 1.1 %fusion.23 = f32[4,2048]{1,0:T(4,128)S(1)} fusion(s32[2048]{0:T(1024)} %bitcast.45, f32[1,128]{1,0:T(1,128)} %bitcast.46, f32[3,128]{1,0:T(4,128)S(1)} %broadcast_multiply_fusion.1), kind=kOutput, calls=%fused_computation.24 | convolution fusion | flops 12845568 | bytes 43008 | tf_op jit(solution)/shard_map/dot_general | solution.py:81
  8.6 0.1 broadcast_in_dim.18
  8.7 0.1 reshape.228
  8.8 0.1 concatenate.36
  9.0 0.3 copy-done.2
  9.4 0.1 concatenate.37
  9.7 0.8 %copy.112 = f32[128,1,128]{2,1,0:T(1,128)} copy(f32[128,1,128]{0,2,1:T(8,128)S(1)} %bitcast.38) | data formatting | bytes 131072 | tf_op jit(solution)/shard_map/all_to_all | solution.py:89
  10.5 9.2 %all-to-all-start = ((f32[128,1,128]{2,1,0:T(1,128)}), f32[128,1,128]{2,1,0:T(1,128)S(1)}, u32[]{:S(2)}, u32[]{:S(2)}) async-start(f32[128,1,128]{2,1,0:T(1,128)} %copy.112), calls=%async_computation | async-start | bytes 131072 | tf_op jit(solution)/shard_map/all_to_all | solution.py:89
  19.8 3.0 %collective-permute-start.2 = (f32[3,16,1,256]{3,1,2,0:T(8,128)S(1)}, f32[3,16,1,256]{3,1,2,0:T(8,128)S(1)}, u32[]{:S(2)}, u32[]{:S(2)}) collective-permute-start(f32[3,16,1,256]{3,1,2,0:T(8,128)S(1)} %get-tuple-element.18), channel_id=1, source_target_pairs={{8,0},{16,8},{24,16},{32,24},{40,32},{48,40},{56,48},{64,56},{72,6... | collective-permute-start | bytes 147464 | tf_op jit(solution)/shard_map/ppermute | solution.py:24
  22.7 4.1 %collective-permute-start.3 = (f32[3,16,1,256]{3,1,2,0:T(8,128)S(1)}, f32[3,16,1,256]{3,1,2,0:T(8,128)S(1)}, u32[]{:S(2)}, u32[]{:S(2)}) collective-permute-start(f32[3,16,1,256]{3,1,2,0:T(8,128)S(1)} %get-tuple-element.19), channel_id=1, source_target_pairs={{0,8},{8,16},{16,24},{24,32},{32,40},{40,48},{48,56},{56,64},{64,7... | collective-permute-start | bytes 147464 | tf_op jit(solution)/shard_map/ppermute | solution.py:21
  26.9 0.1 fusion.63
  27.1 0.6 copy-done.3
  27.9 1.6 %all-to-all-done = f32[128,1,128]{2,1,0:T(1,128)S(1)} async-done(((f32[128,1,128]{2,1,0:T(1,128)}), f32[128,1,128]{2,1,0:T(1,128)S(1)}, u32[]{:S(2)}, u32[]{:S(2)}) %all-to-all-start) | async-done | bytes 65568 | tf_op jit(solution)/shard_map/all_to_all | solution.py:89
  29.6 0.1 copy.116
  29.8 0.1 copy.117
  30.0 0.1 copy.115
  30.2 0.1 copy.114
  30.3 0.1 slice.84
  30.6 0.1 copy.118
  30.9 3.0 %fusion.32 = f32[3,16,4,256]{3,1,2,0:T(8,128)S(1)} fusion(f32[3,16,4,256]{3,1,2,0:T(8,128)S(1)} %copy.134, f32[3,16,1,256]{3,1,2,0:T(8,128)S(1)} %collective-permute-done.3, f32[3,16,1,256]{3,1,2,0:T(8,128)S(1)} %collective-permute-done.2, f32[3,1,4,256]{3,1,2,0:T(1,128)S(1)} %collective-permute-done.1, f32[3,1,4,256]{3,1,2,0:T(1,128)S(1)} %collective-permute-done, ...), kind=kOutput, calls=%fused_computation.34 | convolution fusion | flops 1214955520 | bytes 1556480 | tf_op jit(solution)/shard_map/dot_general | solution.py:46
  33.8 0.1 copy.135
  34.0 14.7 %all_to_all.30 = f32[3,16,4,256]{3,2,0,1:T(4,128)S(1)} all-to-all(f32[3,16,4,256]{3,2,0,1:T(4,128)S(1)} %copy.135), channel_id=1, replica_groups=mesh['gx'=16,'gy'=8] {'gx'}, dimensions={1} | all-to-all | bytes 393216 | tf_op jit(solution)/shard_map/all_to_all | solution.py:105
  48.8 0.3 convolution_bitcast_fusion
  49.1 0.2 copy.137
  49.3 11.4 %all_to_all.31 = f32[3,1,64,256]{3,1,0,2:T(1,128)S(1)} all-to-all(f32[3,1,64,256]{3,1,0,2:T(1,128)S(1)} %copy.137), channel_id=1, replica_groups=mesh['gx'=16,'gy'=8] {'gx'}, dimensions={2} | all-to-all | bytes 393216 | tf_op jit(solution)/shard_map/all_to_all | solution.py:107
  60.8 0.7 %all_to_all.26 = f32[3,16,4,256]{3,2,1,0:T(4,128)} reshape(f32[3,1,64,256]{3,2,0,1:T(8,128)S(1)} %copy.138) | data formatting | bytes 393216 | tf_op jit(solution)/shard_map/all_to_all | solution.py:107
  (49 shorter events, 1.6 us)
Async XLA Ops:
  0.0 48.8 %copy-start = (f32[64,64]{1,0:T(8,128)S(1)}, f32[64,64]{1,0:T(8,128)}, u32[]{:S(2)}) copy-start(f32[64,64]{1,0:T(8,128)} %param.17) | copy-start | bytes 49156
  0.0 8.6 %copy-start.4 = (s32[1,128]{1,0:T(1,128)S(1)}, s32[1,128]{1,0:T(1,128)}, u32[]{:S(2)}) copy-start(s32[1,128]{1,0:T(1,128)} %param.14) | copy-start | bytes 1540
  0.8 30.1 %collective-permute-start.1 = (f32[3,1,4,256]{3,1,2,0:T(1,128)S(1)}, f32[3,1,4,256]{3,1,2,0:T(1,128)S(1)}, u32[]{:S(2)}, u32[]{:S(2)}) collective-permute-start(f32[3,1,4,256]{3,1,2,0:T(1,128)S(1)} %copy.121), channel_id=1, source_target_pairs={{0,1},{1,2},{2,3},{3,4},{4,5},{5,6},{6,7},{7,0},{8,9},{9,10},{10,1... | collective-permute-start | bytes 36872 | tf_op jit(solution)/shard_map/ppermute | solution.py:21
  2.9 28.0 %collective-permute-start = (f32[3,1,4,256]{3,1,2,0:T(1,128)S(1)}, f32[3,1,4,256]{3,1,2,0:T(1,128)S(1)}, u32[]{:S(2)}, u32[]{:S(2)}) collective-permute-start(f32[3,1,4,256]{3,1,2,0:T(1,128)S(1)} %copy.119), channel_id=1, source_target_pairs={{1,0},{2,1},{3,2},{4,3},{5,4},{6,5},{7,6},{0,7},{9,8},{10,9},{11,1... | collective-permute-start | bytes 36872 | tf_op jit(solution)/shard_map/ppermute | solution.py:24
  8.6 0.7 %copy-start.2 = (f32[3,1,2048]{2,1,0:T(1,128)S(1)}, f32[3,1,2048]{2,1,0:T(1,128)}, u32[]{:S(2)}) copy-start(f32[3,1,2048]{2,1,0:T(1,128)} %param.15) | copy-start | bytes 73732
  9.4 10.3 %copy-start.1 = (f32[3,16,4,256]{3,2,1,0:T(4,128)S(1)}, f32[3,16,4,256]{3,2,1,0:T(4,128)}, u32[]{:S(2)}) copy-start(f32[3,16,4,256]{3,2,1,0:T(4,128)} %param.9) | copy-start | bytes 589828
  10.5 19.0 %all-to-all-start = ((f32[128,1,128]{2,1,0:T(1,128)}), f32[128,1,128]{2,1,0:T(1,128)S(1)}, u32[]{:S(2)}, u32[]{:S(2)}) async-start(f32[128,1,128]{2,1,0:T(1,128)} %copy.112), calls=%async_computation | async-start | bytes 131072 | tf_op jit(solution)/shard_map/all_to_all | solution.py:89
  19.8 11.1 %collective-permute-start.2 = (f32[3,16,1,256]{3,1,2,0:T(8,128)S(1)}, f32[3,16,1,256]{3,1,2,0:T(8,128)S(1)}, u32[]{:S(2)}, u32[]{:S(2)}) collective-permute-start(f32[3,16,1,256]{3,1,2,0:T(8,128)S(1)} %get-tuple-element.18), channel_id=1, source_target_pairs={{8,0},{16,8},{24,16},{32,24},{40,32},{48,40},{56,48},{64,56},{72,6... | collective-permute-start | bytes 147464 | tf_op jit(solution)/shard_map/ppermute | solution.py:24
  22.7 8.1 %collective-permute-start.3 = (f32[3,16,1,256]{3,1,2,0:T(8,128)S(1)}, f32[3,16,1,256]{3,1,2,0:T(8,128)S(1)}, u32[]{:S(2)}, u32[]{:S(2)}) collective-permute-start(f32[3,16,1,256]{3,1,2,0:T(8,128)S(1)} %get-tuple-element.19), channel_id=1, source_target_pairs={{0,8},{8,16},{16,24},{24,32},{32,40},{40,48},{48,56},{56,64},{64,7... | collective-permute-start | bytes 147464 | tf_op jit(solution)/shard_map/ppermute | solution.py:21
  26.9 0.7 %copy-start.3 = (s32[1,2048]{1,0:T(1,128)S(1)}, s32[1,2048]{1,0:T(1,128)}, u32[]{:S(2)}) copy-start(s32[1,2048]{1,0:T(1,128)} %param.16) | copy-start | bytes 24580

commit v3 on v2

--- a/solution.py
+++ b/solution.py
@@ -3,7 +3,60 @@
 import jax
 import jax.numpy as jnp
 from jax import lax
+from jax.experimental import pallas as pl
 from jax.sharding import PartitionSpec as P
+
+HIGHEST = lax.Precision.HIGHEST
+
+
+def _rows(pieces, shape):
+    row = lax.broadcasted_iota(jnp.int32, shape, 0)
+    total = jnp.zeros(shape, jnp.float32)
+    for k, piece in enumerate(pieces):
+        total = jnp.where(row == k, jnp.broadcast_to(piece, shape), total)
+    return total
+
+
+def source_kernel(pv_ref, coef_ref, width_ref, sp_ref, cnt_ref, off_ref, out_ref):
+    points = pv_ref.shape[1]
+    slots = sp_ref.shape[1]
+    tiles = cnt_ref.shape[1]
+    capacity = slots // tiles
+    fields = out_ref.shape[1] // capacity
+    pv = pv_ref[...]
+    speed = jnp.sqrt(pv[0:1] * pv[0:1] + pv[1:2] * pv[1:2] + pv[2:3] * pv[2:3])
+    force = -(coef_ref[...] * speed) * pv
+    vals = _rows([force[0:1], force[1:2], force[2:3], width_ref[...]], (8, points))
+    pick = (lax.broadcasted_iota(jnp.int32, (points, slots), 0) == sp_ref[...]).astype(jnp.float32)
+    picked = jnp.dot(vals, pick, precision=HIGHEST, preferred_element_type=jnp.float32)
+    slot_at = lax.broadcasted_iota(jnp.int32, (tiles, slots), 1)
+    tile_at = lax.broadcasted_iota(jnp.int32, (tiles, slots), 0)
+    tile_of = (slot_at // capacity == tile_at).astype(jnp.float32)
+    counts = _rows([cnt_ref[...].astype(jnp.float32)], (8, tiles))
+    limit = jnp.dot(counts, tile_of, precision=HIGHEST, preferred_element_type=jnp.float32)[0:1]
+    lane = (lax.broadcasted_iota(jnp.int32, (1, slots), 1) % capacity).astype(jnp.float32)
+    live = jnp.where(lane < limit, 1.0, 0.0)
+    off = off_ref[...]
+    table = _rows([picked[0:1] * live, picked[1:2] * live, picked[2:3] * live,
+                   off[0:1], off[1:2], off[2:3], picked[3:4]], (fields, slots))
+    lanes_out = fields * capacity
+    field_of = (lax.broadcasted_iota(jnp.int32, (lanes_out, fields), 0) // capacity
+                == lax.broadcasted_iota(jnp.int32, (lanes_out, fields), 1)).astype(jnp.float32)
+    spread = jnp.dot(field_of, table, precision=HIGHEST, preferred_element_type=jnp.float32)
+    same_c = (lax.broadcasted_iota(jnp.int32, (lanes_out, slots), 1) % capacity
+              == lax.broadcasted_iota(jnp.int32, (lanes_out, slots), 0) % capacity)
+    spread = jnp.where(same_c, spread, 0.0)
+    out_ref[...] = lax.dot_general(tile_of, spread, (((1,), (1,)), ((), ())), precision=HIGHEST,
+                                   preferred_element_type=jnp.float32)
+
+
+def source_records(pv, coef, width, sp, cnt, off):
+    tiles = cnt.shape[1]
+    capacity = sp.shape[1] // tiles
+    return pl.pallas_call(
+        source_kernel,
+        out_shape=jax.ShapeDtypeStruct((tiles, 8 * capacity), jnp.float32),
+    )(pv, coef, width, sp, cnt, off)
 
 K = 4
 
@@ -70,22 +123,15 @@
     slot_total = send_point.shape[1]
     device_count = lax.axis_size("gx") * lax.axis_size("gy")
     capacity = slot_total // device_count
-    point_speed = jnp.sqrt(jnp.sum(point_velocity * point_velocity, axis=0))
-    point_force = -(point_coef * point_speed)[None, :] * point_velocity
-    chosen = send_point[0]
-    limits = jnp.repeat(send_count[0], capacity)
-    within = jnp.arange(slot_total, dtype=jnp.int32) % capacity < limits
-    point_count = point_velocity.shape[1]
-    pick = (jnp.arange(point_count, dtype=jnp.int32)[:, None] == chosen[None, :]).astype(jnp.float32)
-    point_values = jnp.concatenate([point_force, point_width[None, :]], axis=0)
-    picked = jnp.dot(point_values, pick, precision=lax.Precision.HIGHEST, preferred_element_type=jnp.float32)
-    slot_force = picked[0:3] * within.astype(jnp.float32)[None, :]
-    slot_width = picked[3:4]
-    spare = jnp.zeros_like(slot_width)
-    records = jnp.concatenate([slot_force, slot_offset[:, 0, :], slot_width, spare], axis=0)
-    fields = records.shape[0]
-    records = records.reshape(fields, device_count, capacity).transpose(1, 0, 2)
-    records = records.reshape(device_count, fields * capacity)
+    records = source_records(
+        point_velocity,
+        point_coef[None, :],
+        point_width[None, :],
+        send_point,
+        send_count,
+        slot_offset[:, 0, :],
+    )
+    fields = records.shape[1] // capacity
     arrived = lax.all_to_all(records, ("gx", "gy"), split_axis=0, concat_axis=0, tiled=True)
     arrived = arrived.reshape(device_count, fields, capacity).transpose(1, 0, 2)
     arrived = arrived.reshape(fields, slot_total)

time: 62 us -> 62.5 us (level)
  Pallas kernels: 0 us -> 4.44 us
  other arithmetic: 2.53 us -> 0.32 us
  matrix products: 4.42 us -> 3.27 us
    pallas_call x0 -> x1, Pallas kernels: none -> 4.44 us  [source_records(): pl.pallas_call(source_kernel, out_shape=jax.ShapeDtypeStruct((tiles, 8 *...]
    dot_general x1 -> x0, matrix products: 1.14 us -> none  [local(): jnp.dot(point_values, pick, precision=lax.Precision.HIGHEST, preferred_el...]
    unnamed x11 -> x8, local copies, waits for them, and re-layouts: 0.89 us -> 1.98 us
    all_to_all x2 -> x1, local copies, waits for them, and re-layouts: 0.84 us -> 0.09 us  [local(): lax.all_to_all(records, ('gx', 'gy'), split_axis=0, concat_axis=0, tiled=...]
    mul x2 -> x0, other arithmetic: 0.7 us -> none  [the longest x1 0.69 us: local(): point_force = -(point_coef * point_speed)[None, :] * point_velocity]
    reduce_sum x1 -> x0, other arithmetic: 0.7 us -> none  [local(): point_speed = jnp.sqrt(jnp.sum(point_velocity * point_velocity, axis=0))]
    neg x1 -> x0, other arithmetic: 0.66 us -> none  [local(): point_force = -(point_coef * point_speed)[None, :] * point_velocity]
  transfers between devices with their start and end apart: 5 -> 5, of which waited for: 1 -> 1; matrix products, arithmetic and copies ran while one was open for 11% -> 5% of each run, Pallas kernels for 0% -> 7%
where the time goes in v3:
time: 62.5 us; the launch traced here: 62.1 us
  blocking collectives  26.1 us (42%)
  starting transfers between devices  20.7 us (33%)
  local copies, waits for them, and re-layouts  5.29 us (8%)
  Pallas kernels  4.44 us (7%)
  matrix products  3.27 us (5%)
  waiting for transfers between devices  1.63 us (3%)
    all_to_all x1, blocking collectives, local(): lax.all_to_all(updated, 'gx', split_axis=1, concat_axis=2, tiled=True)  14.7 us
    all_to_all x1, blocking collectives, local(): lax.all_to_all(solved, 'gx', split_axis=2, concat_axis=1, tiled=True)  11.4 us
    all_to_all x1, starting transfers between devices, local(): lax.all_to_all(records, ('gx', 'gy'), split_axis=0, concat_axis=0, tiled=...  9.18 us
    ppermute x2, starting transfers between devices, with_halo(): lax.ppermute(lax.slice_in_dim(block, block.shape[dim] - width, None, axis...  6.19 us
    ppermute x2, starting transfers between devices, with_halo(): lax.ppermute(lax.slice_in_dim(block, 0, width, axis=dim), axis, backward)  5.34 us
    pallas_call x1, Pallas kernels, source_records(): pl.pallas_call(source_kernel, out_shape=jax.ShapeDtypeStruct((tiles, 8 *...  4.44 us
    dot_general x1, matrix products, deposit_blocks(): lax.dot_general(left, along_y, (((1,), (1,)), ((), ())), precision=lax.Pr...  2.96 us
    unnamed x8, local copies, waits for them, and re-layouts  1.98 us
  transfers between devices with their start and end apart: 5, of which 1 were waited for; matrix products, arithmetic and copies ran while one was open for 5% of the time, Pallas kernels for 7%

profile of v3, /device:TPU:1, one launch (start us, length us, event | category | flops | bytes accessed | tf_op | source)
XLA Modules:
  0.0 62.1 jit_solution(11963225986627252818)
XLA Ops:
  0.0 0.8 %fusion.53 = (f32[3,1,4,256]{3,2,1,0:T(4,128)S(1)}, f32[3,1,4,256]{3,2,1,0:T(4,128)S(1)}) fusion(f32[3,16,4,256]{3,2,1,0:T(4,128)} %param.9), kind=kLoop, calls=%fused_computation.76 | loop fusion | bytes 49152 | tf_op jit(solution)/shard_map/slice | solution.py:77
  0.8 2.1 %collective-permute-start.1 = (f32[3,1,4,256]{3,1,2,0:T(1,128)S(1)}, f32[3,1,4,256]{3,1,2,0:T(1,128)S(1)}, u32[]{:S(2)}, u32[]{:S(2)}) collective-permute-start(f32[3,1,4,256]{3,1,2,0:T(1,128)S(1)} %copy.112), channel_id=1, source_target_pairs={{0,1},{1,2},{2,3},{3,4},{4,5},{5,6},{6,7},{7,0},{8,9},{9,10},{10,1... | collective-permute-start | bytes 36872 | tf_op jit(solution)/shard_map/ppermute | solution.py:74
  2.9 2.4 %collective-permute-start = (f32[3,1,4,256]{3,1,2,0:T(1,128)S(1)}, f32[3,1,4,256]{3,1,2,0:T(1,128)S(1)}, u32[]{:S(2)}, u32[]{:S(2)}) collective-permute-start(f32[3,1,4,256]{3,1,2,0:T(1,128)S(1)} %copy.110), channel_id=1, source_target_pairs={{1,0},{2,1},{3,2},{4,3},{5,4},{6,5},{7,6},{0,7},{9,8},{10,9},{11,1... | collective-permute-start | bytes 36872 | tf_op jit(solution)/shard_map/ppermute | solution.py:77
  5.3 1.4 %copy.133 = f32[3,1,2048]{2,0,1:T(4,128)} copy(f32[3,1,2048]{2,1,0:T(1,128)} %param.15) | data formatting | bytes 49152
  6.6 4.4 %shard_map.91 = f32[128,128]{1,0:T(8,128)} custom-call(f32[3,128]{1,0:T(4,128)} %pv_ref.1, f32[1,128]{1,0:T(1,128)} %bitcast.46, f32[1,128]{1,0:T(1,128)} %bitcast.47, s32[1,2048]{1,0:T(1,128)} %sp_ref.1, s32[1,128]{1,0:T(1,128)} %cnt_ref.1, f32[3,2048]{1,0:T(4,128)} %bitcast.42), custom_call_target="tpu_custom_call" | custom-call | tf_op jit(solution)/shard_map/pallas_call | solution.py:56
  11.1 9.2 %all-to-all-start = ((f32[128,1,128]{2,1,0:T(1,128)}), f32[128,1,128]{2,1,0:T(1,128)S(1)}, u32[]{:S(2)}, u32[]{:S(2)}) async-start(f32[128,1,128]{2,1,0:T(1,128)} %bitcast.39), calls=%async_computation | async-start | bytes 131072 | tf_op jit(solution)/shard_map/all_to_all | solution.py:135
  20.3 3.0 %collective-permute-start.2 = (f32[3,16,1,256]{3,1,2,0:T(8,128)S(1)}, f32[3,16,1,256]{3,1,2,0:T(8,128)S(1)}, u32[]{:S(2)}, u32[]{:S(2)}) collective-permute-start(f32[3,16,1,256]{3,1,2,0:T(8,128)S(1)} %get-tuple-element.18), channel_id=1, source_target_pairs={{8,0},{16,8},{24,16},{32,24},{40,32},{48,40},{56,48},{64,56},{72,6... | collective-permute-start | bytes 147464 | tf_op jit(solution)/shard_map/ppermute | solution.py:77
  23.3 4.1 %collective-permute-start.3 = (f32[3,16,1,256]{3,1,2,0:T(8,128)S(1)}, f32[3,16,1,256]{3,1,2,0:T(8,128)S(1)}, u32[]{:S(2)}, u32[]{:S(2)}) collective-permute-start(f32[3,16,1,256]{3,1,2,0:T(8,128)S(1)} %get-tuple-element.19), channel_id=1, source_target_pairs={{0,8},{8,16},{16,24},{24,32},{32,40},{40,48},{48,56},{56,64},{64,7... | collective-permute-start | bytes 147464 | tf_op jit(solution)/shard_map/ppermute | solution.py:74
  27.4 0.1 fusion.51
  27.5 0.1 fusion.52
  27.6 0.6 copy-done.2
  28.5 1.6 %all-to-all-done = f32[128,1,128]{2,1,0:T(1,128)S(1)} async-done(((f32[128,1,128]{2,1,0:T(1,128)}), f32[128,1,128]{2,1,0:T(1,128)S(1)}, u32[]{:S(2)}, u32[]{:S(2)}) %all-to-all-start) | async-done | bytes 65568 | tf_op jit(solution)/shard_map/all_to_all | solution.py:135
  30.1 0.1 copy.104
  30.2 0.1 copy.107
  30.3 0.1 sub.116
  30.4 0.1 copy.108
  30.5 0.1 sub.123
  30.6 0.1 copy.106
  30.7 0.1 squeeze.8
  30.8 0.1 copy.105
  30.9 0.1 slice.76
  31.1 0.1 exponential_select_fusion
  31.2 0.1 copy.109
  31.3 0.1 sub.130
  31.5 3.0 %fusion.30 = f32[3,16,4,256]{3,1,2,0:T(8,128)S(1)} fusion(f32[3,16,4,256]{3,1,2,0:T(8,128)S(1)} %copy.125, f32[3,16,1,256]{3,1,2,0:T(8,128)S(1)} %collective-permute-done.3, f32[3,16,1,256]{3,1,2,0:T(8,128)S(1)} %collective-permute-done.2, f32[3,1,4,256]{3,1,2,0:T(1,128)S(1)} %collective-permute-done.1, f32[3,1,4,256]{3,1,2,0:T(1,128)S(1)} %collective-permute-done, ...), kind=kOutput, calls=%fused_computation.31 | convolution fusion | flops 1214955520 | bytes 1556480 | tf_op jit(solution)/shard_map/dot_general | solution.py:99
  34.4 0.1 copy.126
  34.6 14.7 %all_to_all.30 = f32[3,16,4,256]{3,2,0,1:T(4,128)S(1)} all-to-all(f32[3,16,4,256]{3,2,0,1:T(4,128)S(1)} %copy.126), channel_id=1, replica_groups=mesh['gx'=16,'gy'=8] {'gx'}, dimensions={1} | all-to-all | bytes 393216 | tf_op jit(solution)/shard_map/all_to_all | solution.py:151
  49.3 0.1 reshape.201
  49.4 0.3 convolution_bitcast_fusion
  49.7 0.2 copy.128
  49.9 11.4 %all_to_all.31 = f32[3,1,64,256]{3,1,0,2:T(1,128)S(1)} all-to-all(f32[3,1,64,256]{3,1,0,2:T(1,128)S(1)} %copy.128), channel_id=1, replica_groups=mesh['gx'=16,'gy'=8] {'gx'}, dimensions={2} | all-to-all | bytes 393216 | tf_op jit(solution)/shard_map/all_to_all | solution.py:153
  61.3 0.7 %all_to_all.26 = f32[3,16,4,256]{3,2,1,0:T(4,128)} reshape(f32[3,1,64,256]{3,2,0,1:T(8,128)S(1)} %copy.129) | data formatting | bytes 393216 | tf_op jit(solution)/shard_map/all_to_all | solution.py:153
  (28 shorter events, 0.4 us)
Async XLA Ops:
  0.0 49.4 %copy-start = (f32[64,64]{1,0:T(8,128)S(1)}, f32[64,64]{1,0:T(8,128)}, u32[]{:S(2)}) copy-start(f32[64,64]{1,0:T(8,128)} %param.17) | copy-start | bytes 49156
  0.0 20.3 %copy-start.1 = (f32[3,16,4,256]{3,2,1,0:T(4,128)S(1)}, f32[3,16,4,256]{3,2,1,0:T(4,128)}, u32[]{:S(2)}) copy-start(f32[3,16,4,256]{3,2,1,0:T(4,128)} %param.9) | copy-start | bytes 589828
  0.8 30.6 %collective-permute-start.1 = (f32[3,1,4,256]{3,1,2,0:T(1,128)S(1)}, f32[3,1,4,256]{3,1,2,0:T(1,128)S(1)}, u32[]{:S(2)}, u32[]{:S(2)}) collective-permute-start(f32[3,1,4,256]{3,1,2,0:T(1,128)S(1)} %copy.112), channel_id=1, source_target_pairs={{0,1},{1,2},{2,3},{3,4},{4,5},{5,6},{6,7},{7,0},{8,9},{9,10},{10,1... | collective-permute-start | bytes 36872 | tf_op jit(solution)/shard_map/ppermute | solution.py:74
  2.9 28.5 %collective-permute-start = (f32[3,1,4,256]{3,1,2,0:T(1,128)S(1)}, f32[3,1,4,256]{3,1,2,0:T(1,128)S(1)}, u32[]{:S(2)}, u32[]{:S(2)}) collective-permute-start(f32[3,1,4,256]{3,1,2,0:T(1,128)S(1)} %copy.110), channel_id=1, source_target_pairs={{1,0},{2,1},{3,2},{4,3},{5,4},{6,5},{7,6},{0,7},{9,8},{10,9},{11,1... | collective-permute-start | bytes 36872 | tf_op jit(solution)/shard_map/ppermute | solution.py:77
  11.1 19.0 %all-to-all-start = ((f32[128,1,128]{2,1,0:T(1,128)}), f32[128,1,128]{2,1,0:T(1,128)S(1)}, u32[]{:S(2)}, u32[]{:S(2)}) async-start(f32[128,1,128]{2,1,0:T(1,128)} %bitcast.39), calls=%async_computation | async-start | bytes 131072 | tf_op jit(solution)/shard_map/all_to_all | solution.py:135
  20.3 11.1 %collective-permute-start.2 = (f32[3,16,1,256]{3,1,2,0:T(8,128)S(1)}, f32[3,16,1,256]{3,1,2,0:T(8,128)S(1)}, u32[]{:S(2)}, u32[]{:S(2)}) collective-permute-start(f32[3,16,1,256]{3,1,2,0:T(8,128)S(1)} %get-tuple-element.18), channel_id=1, source_target_pairs={{8,0},{16,8},{24,16},{32,24},{40,32},{48,40},{56,48},{64,56},{72,6... | collective-permute-start | bytes 147464 | tf_op jit(solution)/shard_map/ppermute | solution.py:77
  23.3 8.1 %collective-permute-start.3 = (f32[3,16,1,256]{3,1,2,0:T(8,128)S(1)}, f32[3,16,1,256]{3,1,2,0:T(8,128)S(1)}, u32[]{:S(2)}, u32[]{:S(2)}) collective-permute-start(f32[3,16,1,256]{3,1,2,0:T(8,128)S(1)} %get-tuple-element.19), channel_id=1, source_target_pairs={{0,8},{8,16},{16,24},{24,32},{32,40},{40,48},{48,56},{56,64},{64,7... | collective-permute-start | bytes 147464 | tf_op jit(solution)/shard_map/ppermute | solution.py:74
  27.5 0.7 %copy-start.2 = (s32[1,2048]{1,0:T(1,128)S(1)}, s32[1,2048]{1,0:T(1,128)}, u32[]{:S(2)}) copy-start(s32[1,2048]{1,0:T(1,128)} %param.16) | copy-start | bytes 24580

commit v4 on v3

--- a/solution.py
+++ b/solution.py
@@ -22,7 +22,7 @@
     slots = sp_ref.shape[1]
     tiles = cnt_ref.shape[1]
     capacity = slots // tiles
-    fields = out_ref.shape[1] // capacity
+    fields = out_ref.shape[0]
     pv = pv_ref[...]
     speed = jnp.sqrt(pv[0:1] * pv[0:1] + pv[1:2] * pv[1:2] + pv[2:3] * pv[2:3])
     force = -(coef_ref[...] * speed) * pv
@@ -33,30 +33,20 @@
     tile_at = lax.broadcasted_iota(jnp.int32, (tiles, slots), 0)
     tile_of = (slot_at // capacity == tile_at).astype(jnp.float32)
     counts = _rows([cnt_ref[...].astype(jnp.float32)], (8, tiles))
-    limit = jnp.dot(counts, tile_of, precision=HIGHEST, preferred_element_type=jnp.float32)[0:1]
+    limit = jnp.dot(counts, tile_of, preferred_element_type=jnp.float32)[0:1]
     lane = (lax.broadcasted_iota(jnp.int32, (1, slots), 1) % capacity).astype(jnp.float32)
     live = jnp.where(lane < limit, 1.0, 0.0)
-    off = off_ref[...]
-    table = _rows([picked[0:1] * live, picked[1:2] * live, picked[2:3] * live,
-                   off[0:1], off[1:2], off[2:3], picked[3:4]], (fields, slots))
-    lanes_out = fields * capacity
-    field_of = (lax.broadcasted_iota(jnp.int32, (lanes_out, fields), 0) // capacity
-                == lax.broadcasted_iota(jnp.int32, (lanes_out, fields), 1)).astype(jnp.float32)
-    spread = jnp.dot(field_of, table, precision=HIGHEST, preferred_element_type=jnp.float32)
-    same_c = (lax.broadcasted_iota(jnp.int32, (lanes_out, slots), 1) % capacity
-              == lax.broadcasted_iota(jnp.int32, (lanes_out, slots), 0) % capacity)
-    spread = jnp.where(same_c, spread, 0.0)
-    out_ref[...] = lax.dot_general(tile_of, spread, (((1,), (1,)), ((), ())), precision=HIGHEST,
-                                   preferred_element_type=jnp.float32)
+    out_ref[...] = _rows([picked[0:1] * live, picked[1:2] * live, picked[2:3] * live,
+                          off_ref[0, 0:1, :], off_ref[1, 0:1, :], off_ref[2, 0:1, :], picked[3:4]],
+                         (fields, slots))
 
 
 def source_records(pv, coef, width, sp, cnt, off):
-    tiles = cnt.shape[1]
-    capacity = sp.shape[1] // tiles
     return pl.pallas_call(
         source_kernel,
-        out_shape=jax.ShapeDtypeStruct((tiles, 8 * capacity), jnp.float32),
+        out_shape=jax.ShapeDtypeStruct((8, sp.shape[1]), jnp.float32),
     )(pv, coef, width, sp, cnt, off)
+
 
 K = 4
 
@@ -129,9 +119,11 @@
         point_width[None, :],
         send_point,
         send_count,
-        slot_offset[:, 0, :],
+        slot_offset,
     )
-    fields = records.shape[1] // capacity
+    fields = records.shape[0]
+    records = records.reshape(fields, device_count, capacity).transpose(1, 0, 2)
+    records = records.reshape(device_count, fields * capacity)
     arrived = lax.all_to_all(records, ("gx", "gy"), split_axis=0, concat_axis=0, tiled=True)
     arrived = arrived.reshape(device_count, fields, capacity).transpose(1, 0, 2)
     arrived = arrived.reshape(fields, slot_total)

time: 62.5 us -> 65.7 us (1.051)
  waiting for transfers between devices: 1.63 us -> 8.67 us
  blocking collectives: 26.1 us -> 23.3 us
  Pallas kernels: 4.44 us -> 2.2 us
  local copies, waits for them, and re-layouts: 5.29 us -> 6.86 us
    all_to_all x1, waiting for transfers between devices: 1.62 us -> 8.66 us  [local(): lax.all_to_all(records, ('gx', 'gy'), split_axis=0, concat_axis=0, tiled=...]
    all_to_all x1, blocking collectives: 14.7 us -> 11.9 us  [local(): lax.all_to_all(updated, 'gx', split_axis=1, concat_axis=2, tiled=True)]
    pallas_call x1, Pallas kernels: 4.44 us -> 2.2 us  [source_records(): pl.pallas_call(source_kernel, out_shape=jax.ShapeDtypeStruct((8, sp.shape...]
    all_to_all x1, starting transfers between devices: 9.18 us -> 7.94 us  [local(): lax.all_to_all(records, ('gx', 'gy'), split_axis=0, concat_axis=0, tiled=...]
    reshape x0 -> x1, local copies, waits for them, and re-layouts: none -> 1.04 us  [local(): records = records.reshape(fields, device_count, capacity).transpose(1, 0, 2)]
    ppermute x2, starting transfers between devices: 6.19 us -> 6.93 us  [with_halo(): lax.ppermute(lax.slice_in_dim(block, block.shape[dim] - width, None, axis...]
    all_to_all x1 -> x2, local copies, waits for them, and re-layouts: 0.09 us -> 0.83 us  [local(): lax.all_to_all(records, ('gx', 'gy'), split_axis=0, concat_axis=0, tiled=...]
    unnamed x8 -> x7, local copies, waits for them, and re-layouts: 1.98 us -> 1.65 us
  transfers between devices with their start and end apart: 5 -> 5, of which waited for: 1 -> 1; matrix products, arithmetic and copies ran while one was open for 5% -> 7% of each run, Pallas kernels for 7% -> 3%
where the time goes in v4:
time: 65.7 us; the launch traced here: 65.2 us
  blocking collectives  23.3 us (35%)
  starting transfers between devices  20.3 us (31%)
  waiting for transfers between devices  8.67 us (13%)
  local copies, waits for them, and re-layouts  6.86 us (10%)
  matrix products  3.28 us (5%)
  Pallas kernels  2.2 us (3%)
    all_to_all x1, blocking collectives, local(): lax.all_to_all(updated, 'gx', split_axis=1, concat_axis=2, tiled=True)  11.9 us
    all_to_all x1, blocking collectives, local(): lax.all_to_all(solved, 'gx', split_axis=2, concat_axis=1, tiled=True)  11.4 us
    all_to_all x1, waiting for transfers between devices, local(): lax.all_to_all(records, ('gx', 'gy'), split_axis=0, concat_axis=0, tiled=...  8.66 us
    all_to_all x1, starting transfers between devices, local(): lax.all_to_all(records, ('gx', 'gy'), split_axis=0, concat_axis=0, tiled=...  7.94 us
    ppermute x2, starting transfers between devices, with_halo(): lax.ppermute(lax.slice_in_dim(block, block.shape[dim] - width, None, axis...  6.93 us
    ppermute x2, starting transfers between devices, with_halo(): lax.ppermute(lax.slice_in_dim(block, 0, width, axis=dim), axis, backward)  5.47 us
    dot_general x1, matrix products, deposit_blocks(): lax.dot_general(left, along_y, (((1,), (1,)), ((), ())), precision=lax.Pr...  2.97 us
    pallas_call x1, Pallas kernels, source_records(): pl.pallas_call(source_kernel, out_shape=jax.ShapeDtypeStruct((8, sp.shape...  2.2 us
  transfers between devices with their start and end apart: 5, of which 1 were waited for; matrix products, arithmetic and copies ran while one was open for 7% of the time, Pallas kernels for 3%

profile of v4, /device:TPU:1, one launch (start us, length us, event | category | flops | bytes accessed | tf_op | source)
XLA Modules:
  0.0 65.2 jit_solution(18342205865267963654)
XLA Ops:
  0.0 0.7 %fusion.53 = (f32[3,1,4,256]{3,2,1,0:T(4,128)S(1)}, f32[3,1,4,256]{3,2,1,0:T(4,128)S(1)}) fusion(f32[3,16,4,256]{3,2,1,0:T(4,128)} %param.9), kind=kLoop, calls=%fused_computation.75 | loop fusion | bytes 49152 | tf_op jit(solution)/shard_map/slice | solution.py:67
  0.8 2.1 %collective-permute-start.1 = (f32[3,1,4,256]{3,1,2,0:T(1,128)S(1)}, f32[3,1,4,256]{3,1,2,0:T(1,128)S(1)}, u32[]{:S(2)}, u32[]{:S(2)}) collective-permute-start(f32[3,1,4,256]{3,1,2,0:T(1,128)S(1)} %copy.115), channel_id=1, source_target_pairs={{0,1},{1,2},{2,3},{3,4},{4,5},{5,6},{6,7},{7,0},{8,9},{9,10},{10,1... | collective-permute-start | bytes 36872 | tf_op jit(solution)/shard_map/ppermute | solution.py:64
  2.9 2.4 %collective-permute-start = (f32[3,1,4,256]{3,1,2,0:T(1,128)S(1)}, f32[3,1,4,256]{3,1,2,0:T(1,128)S(1)}, u32[]{:S(2)}, u32[]{:S(2)}) collective-permute-start(f32[3,1,4,256]{3,1,2,0:T(1,128)S(1)} %copy.113), channel_id=1, source_target_pairs={{1,0},{2,1},{3,2},{4,3},{5,4},{6,5},{7,6},{0,7},{9,8},{10,9},{11,1... | collective-permute-start | bytes 36872 | tf_op jit(solution)/shard_map/ppermute | solution.py:67
  5.2 1.0 %copy.128 = f32[3,16,4,256]{3,1,2,0:T(8,128)S(1)} copy(f32[3,16,4,256]{3,2,1,0:T(4,128)} %param.9) | data formatting | bytes 393216 | tf_op args[0]
  6.2 3.1 %collective-permute-start.2 = (f32[3,16,1,256]{3,1,2,0:T(8,128)S(1)}, f32[3,16,1,256]{3,1,2,0:T(8,128)S(1)}, u32[]{:S(2)}, u32[]{:S(2)}) collective-permute-start(f32[3,16,1,256]{3,1,2,0:T(8,128)S(1)} %get-tuple-element.18), channel_id=1, source_target_pairs={{8,0},{16,8},{24,16},{32,24},{40,32},{48,40},{56,48},{64,56},{72,6... | collective-permute-start | bytes 147464 | tf_op jit(solution)/shard_map/ppermute | solution.py:67
  9.3 4.8 %collective-permute-start.3 = (f32[3,16,1,256]{3,1,2,0:T(8,128)S(1)}, f32[3,16,1,256]{3,1,2,0:T(8,128)S(1)}, u32[]{:S(2)}, u32[]{:S(2)}) collective-permute-start(f32[3,16,1,256]{3,1,2,0:T(8,128)S(1)} %get-tuple-element.19), channel_id=1, source_target_pairs={{0,8},{8,16},{16,24},{24,32},{32,40},{40,48},{48,56},{56,64},{64,7... | collective-permute-start | bytes 147464 | tf_op jit(solution)/shard_map/ppermute | solution.py:64
  14.2 2.2 %shard_map.91 = f32[8,2048]{1,0:T(8,128)} custom-call(f32[3,128]{1,0:T(4,128)} %pv_ref.1, f32[1,128]{1,0:T(1,128)} %bitcast.42, f32[1,128]{1,0:T(1,128)} %bitcast.43, s32[1,2048]{1,0:T(1,128)} %sp_ref.1, s32[1,128]{1,0:T(1,128)} %cnt_ref.1, f32[3,1,2048]{2,1,0:T(1,128)} %off_ref.1), custom_call_target="tpu_custom_call" | custom-call | tf_op jit(solution)/shard_map/pallas_call | solution.py:45
  16.4 1.0 %reshape.205 = f32[8,128,16]{2,1,0:T(8,128)S(1)} reshape(f32[8,2048]{1,0:T(8,128)} %shard_map.91) | data formatting | bytes 131072 | tf_op jit(solution)/shard_map/reshape | solution.py:125
  17.4 0.2 copy.105
  17.6 0.7 %copy.106 = f32[128,1,128]{2,1,0:T(1,128)} copy(f32[128,1,128]{0,2,1:T(8,128)S(1)} %bitcast.36) | data formatting | bytes 131072 | tf_op jit(solution)/shard_map/all_to_all | solution.py:127
  18.3 7.9 %all-to-all-start = ((f32[128,1,128]{2,1,0:T(1,128)}), f32[128,1,128]{2,1,0:T(1,128)S(1)}, u32[]{:S(2)}, u32[]{:S(2)}) async-start(f32[128,1,128]{2,1,0:T(1,128)} %copy.106), calls=%async_computation | async-start | bytes 131072 | tf_op jit(solution)/shard_map/all_to_all | solution.py:127
  26.3 0.1 fusion.51
  26.4 0.1 fusion.52
  26.5 0.5 copy-done.2
  27.1 0.2 copy-done.1
  27.4 8.7 %all-to-all-done = f32[128,1,128]{2,1,0:T(1,128)S(1)} async-done(((f32[128,1,128]{2,1,0:T(1,128)}), f32[128,1,128]{2,1,0:T(1,128)S(1)}, u32[]{:S(2)}, u32[]{:S(2)}) %all-to-all-start) | async-done | bytes 65568 | tf_op jit(solution)/shard_map/all_to_all | solution.py:127
  36.1 0.1 copy.107
  36.2 0.1 copy.110
  36.4 0.1 copy.111
  36.5 0.1 sub.123
  36.6 0.1 copy.109
  36.7 0.1 squeeze.4
  36.8 0.1 copy.108
  36.9 0.1 slice.76
  37.2 0.1 copy.112
  37.4 3.0 %fusion.30 = f32[3,16,4,256]{3,1,2,0:T(8,128)S(1)} fusion(f32[3,16,4,256]{3,1,2,0:T(8,128)S(1)} %copy.128, f32[3,16,1,256]{3,1,2,0:T(8,128)S(1)} %collective-permute-done.3, f32[3,16,1,256]{3,1,2,0:T(8,128)S(1)} %collective-permute-done.2, f32[3,1,4,256]{3,1,2,0:T(1,128)S(1)} %collective-permute-done.1, f32[3,1,4,256]{3,1,2,0:T(1,128)S(1)} %collective-permute-done, ...), kind=kOutput, calls=%fused_computation.31 | convolution fusion | flops 1214955520 | bytes 1556480 | tf_op jit(solution)/shard_map/dot_general | solution.py:89
  40.4 0.1 copy.129
  40.6 11.9 %all_to_all.30 = f32[3,16,4,256]{3,2,0,1:T(4,128)S(1)} all-to-all(f32[3,16,4,256]{3,2,0,1:T(4,128)S(1)} %copy.129), channel_id=1, replica_groups=mesh['gx'=16,'gy'=8] {'gx'}, dimensions={1} | all-to-all | bytes 393216 | tf_op jit(solution)/shard_map/all_to_all | solution.py:143
  52.5 0.3 convolution_bitcast_fusion
  52.9 0.2 copy.131
  53.1 11.4 %all_to_all.31 = f32[3,1,64,256]{3,1,0,2:T(1,128)S(1)} all-to-all(f32[3,1,64,256]{3,1,0,2:T(1,128)S(1)} %copy.131), channel_id=1, replica_groups=mesh['gx'=16,'gy'=8] {'gx'}, dimensions={2} | all-to-all | bytes 393216 | tf_op jit(solution)/shard_map/all_to_all | solution.py:145
  64.5 0.7 %all_to_all.26 = f32[3,16,4,256]{3,2,1,0:T(4,128)} reshape(f32[3,1,64,256]{3,2,0,1:T(8,128)S(1)} %copy.132) | data formatting | bytes 393216 | tf_op jit(solution)/shard_map/all_to_all | solution.py:145
  (30 shorter events, 0.7 us)
Async XLA Ops:
  0.0 52.5 %copy-start = (f32[64,64]{1,0:T(8,128)S(1)}, f32[64,64]{1,0:T(8,128)}, u32[]{:S(2)}) copy-start(f32[64,64]{1,0:T(8,128)} %param.17) | copy-start | bytes 49156
  0.8 36.7 %collective-permute-start.1 = (f32[3,1,4,256]{3,1,2,0:T(1,128)S(1)}, f32[3,1,4,256]{3,1,2,0:T(1,128)S(1)}, u32[]{:S(2)}, u32[]{:S(2)}) collective-permute-start(f32[3,1,4,256]{3,1,2,0:T(1,128)S(1)} %copy.115), channel_id=1, source_target_pairs={{0,1},{1,2},{2,3},{3,4},{4,5},{5,6},{6,7},{7,0},{8,9},{9,10},{10,1... | collective-permute-start | bytes 36872 | tf_op jit(solution)/shard_map/ppermute | solution.py:64
  2.9 34.6 %collective-permute-start = (f32[3,1,4,256]{3,1,2,0:T(1,128)S(1)}, f32[3,1,4,256]{3,1,2,0:T(1,128)S(1)}, u32[]{:S(2)}, u32[]{:S(2)}) collective-permute-start(f32[3,1,4,256]{3,1,2,0:T(1,128)S(1)} %copy.113), channel_id=1, source_target_pairs={{1,0},{2,1},{3,2},{4,3},{5,4},{6,5},{7,6},{0,7},{9,8},{10,9},{11,1... | collective-permute-start | bytes 36872 | tf_op jit(solution)/shard_map/ppermute | solution.py:67
  6.2 31.2 %collective-permute-start.2 = (f32[3,16,1,256]{3,1,2,0:T(8,128)S(1)}, f32[3,16,1,256]{3,1,2,0:T(8,128)S(1)}, u32[]{:S(2)}, u32[]{:S(2)}) collective-permute-start(f32[3,16,1,256]{3,1,2,0:T(8,128)S(1)} %get-tuple-element.18), channel_id=1, source_target_pairs={{8,0},{16,8},{24,16},{32,24},{40,32},{48,40},{56,48},{64,56},{72,6... | collective-permute-start | bytes 147464 | tf_op jit(solution)/shard_map/ppermute | solution.py:67
  9.3 28.1 %collective-permute-start.3 = (f32[3,16,1,256]{3,1,2,0:T(8,128)S(1)}, f32[3,16,1,256]{3,1,2,0:T(8,128)S(1)}, u32[]{:S(2)}, u32[]{:S(2)}) collective-permute-start(f32[3,16,1,256]{3,1,2,0:T(8,128)S(1)} %get-tuple-element.19), channel_id=1, source_target_pairs={{0,8},{8,16},{16,24},{24,32},{32,40},{40,48},{48,56},{56,64},{64,7... | collective-permute-start | bytes 147464 | tf_op jit(solution)/shard_map/ppermute | solution.py:64
  18.3 17.8 %all-to-all-start = ((f32[128,1,128]{2,1,0:T(1,128)}), f32[128,1,128]{2,1,0:T(1,128)S(1)}, u32[]{:S(2)}, u32[]{:S(2)}) async-start(f32[128,1,128]{2,1,0:T(1,128)} %copy.106), calls=%async_computation | async-start | bytes 131072 | tf_op jit(solution)/shard_map/all_to_all | solution.py:127
  26.3 0.7 %copy-start.2 = (s32[1,2048]{1,0:T(1,128)S(1)}, s32[1,2048]{1,0:T(1,128)}, u32[]{:S(2)}) copy-start(s32[1,2048]{1,0:T(1,128)} %param.16) | copy-start | bytes 24580
  26.4 0.9 %copy-start.1 = (f32[3,16,4,256]{3,2,1,0:T(4,128)S(1)}, f32[3,16,4,256]{3,2,1,0:T(4,128)}, u32[]{:S(2)}) copy-start(f32[3,16,4,256]{3,2,1,0:T(4,128)} %param.9) | copy-start | bytes 589828

commit v5 on v4

--- a/solution.py
+++ b/solution.py
@@ -5,6 +5,7 @@
 from jax import lax
 from jax.experimental import pallas as pl
 from jax.sharding import PartitionSpec as P
+
 
 HIGHEST = lax.Precision.HIGHEST
 
@@ -90,7 +91,7 @@
         left,
         along_y,
         (((1,), (1,)), ((), ())),
-        precision=lax.Precision.HIGHEST,
+        precision=lax.Precision.HIGH,
         preferred_element_type=jnp.float32,
     )
     return result.reshape(3, rows_x, rows_z, rows_y)
@@ -134,13 +135,16 @@
     corner_y = remainder % rows_y
     forcing = deposit_blocks(arrived, corner_x, corner_z, corner_y, rows_x, rows_z, rows_y, K)
     wide_x = with_halo(velocity, (("gy", 1),), 1, True)
-    wide_z = with_halo(velocity, (("gx", 2),), 1, False)
     grad_x = (wide_x[:, 2:] - wide_x[:, :-2]) * 0.5
-    grad_z = (wide_z[:, :, 2:] - wide_z[:, :, :-2]) * 0.5
     grad_y = (jnp.roll(velocity, -1, axis=3) - jnp.roll(velocity, 1, axis=3)) * 0.5
-    transport = velocity[0:1] * grad_x + velocity[1:2] * grad_y + velocity[2:3] * grad_z
-    updated = velocity + time_step * (forcing - transport)
-    columns = lax.all_to_all(updated, "gx", split_axis=1, concat_axis=2, tiled=True)
+    flat_part = velocity[0:1] * grad_x + velocity[1:2] * grad_y
+    partial = velocity + time_step * (forcing - flat_part)
+    both = jnp.concatenate([velocity, partial], axis=0)
+    columns = lax.all_to_all(both, "gx", split_axis=1, concat_axis=2, tiled=True)
+    column_velocity = columns[0:3]
+    padded = jnp.pad(column_velocity, ((0, 0), (0, 0), (1, 1), (0, 0)))
+    grad_z = (padded[:, :, 2:] - padded[:, :, :-2]) * 0.5
+    columns = columns[3:6] - time_step * (column_velocity[2:3] * grad_z)
     solved = jnp.einsum("zk,cxky->cxzy", vertical_inverse, columns, precision=lax.Precision.HIGHEST)
     new_velocity = lax.all_to_all(solved, "gx", split_axis=2, concat_axis=1, tiled=True)
     return new_velocity
@@ -158,6 +162,7 @@
         P(("gx", "gy"), None),
         P(),
     )
+
     return jax.shard_map(
         local, mesh=mesh, in_specs=placed, out_specs=P(None, "gy", "gx", None), check_vma=False
     )

time: 65.7 us -> 59.5 us (0.906)
  starting transfers between devices: 20.3 us -> 13.6 us
  blocking collectives: 23.3 us -> 25.3 us
  local copies, waits for them, and re-layouts: 6.86 us -> 5.98 us
  matrix products: 3.28 us -> 2.42 us
    ppermute x2 -> x1, starting transfers between devices: 6.93 us -> 2.1 us  [with_halo(): lax.ppermute(lax.slice_in_dim(block, block.shape[dim] - width, None, axis...]
    ppermute x2 -> x1, starting transfers between devices: 5.47 us -> 2.37 us  [with_halo(): lax.ppermute(lax.slice_in_dim(block, 0, width, axis=dim), axis, backward)]
    all_to_all x1, blocking collectives: 11.9 us -> 13.5 us  [local(): lax.all_to_all(both, 'gx', split_axis=1, concat_axis=2, tiled=True)]
    all_to_all x1, starting transfers between devices: 7.94 us -> 9.18 us  [local(): lax.all_to_all(records, ('gx', 'gy'), split_axis=0, concat_axis=0, tiled=...]
    unnamed x7, local copies, waits for them, and re-layouts: 1.65 us -> 0.53 us
    dot_general x1, matrix products: 2.97 us -> 2.06 us  [deposit_blocks(): lax.dot_general(left, along_y, (((1,), (1,)), ((), ())), precision=lax.Pr...]
  transfers between devices with their start and end apart: 5 -> 3, of which waited for: 1 -> 1; matrix products, arithmetic and copies ran while one was open for 7% -> 6% of each run, Pallas kernels for 3% -> 4%
where the time goes in v5:
time: 59.5 us; the launch traced here: 59.1 us
  blocking collectives  25.3 us (43%)
  starting transfers between devices  13.6 us (23%)
  waiting for transfers between devices  8.85 us (15%)
  local copies, waits for them, and re-layouts  5.98 us (10%)
  matrix products  2.42 us (4%)
  Pallas kernels  2.2 us (4%)
    all_to_all x1, blocking collectives, local(): lax.all_to_all(both, 'gx', split_axis=1, concat_axis=2, tiled=True)  13.5 us
    all_to_all x1, blocking collectives, local(): lax.all_to_all(solved, 'gx', split_axis=2, concat_axis=1, tiled=True)  11.9 us
    all_to_all x1, starting transfers between devices, local(): lax.all_to_all(records, ('gx', 'gy'), split_axis=0, concat_axis=0, tiled=...  9.18 us
    all_to_all x1, waiting for transfers between devices, local(): lax.all_to_all(records, ('gx', 'gy'), split_axis=0, concat_axis=0, tiled=...  8.84 us
    ppermute x1, starting transfers between devices, with_halo(): lax.ppermute(lax.slice_in_dim(block, 0, width, axis=dim), axis, backward)  2.37 us
    pallas_call x1, Pallas kernels, source_records(): pl.pallas_call(source_kernel, out_shape=jax.ShapeDtypeStruct((8, sp.shape...  2.2 us
    ppermute x1, starting transfers between devices, with_halo(): lax.ppermute(lax.slice_in_dim(block, block.shape[dim] - width, None, axis...  2.1 us
    dot_general x1, matrix products, deposit_blocks(): lax.dot_general(left, along_y, (((1,), (1,)), ((), ())), precision=lax.Pr...  2.06 us
  transfers between devices with their start and end apart: 3, of which 1 were waited for; matrix products, arithmetic and copies ran while one was open for 6% of the time, Pallas kernels for 4%

profile of v5, /device:TPU:1, one launch (start us, length us, event | category | flops | bytes accessed | tf_op | source)
XLA Modules:
  0.0 59.1 jit_solution(14214030465558373103)
XLA Ops:
  0.0 0.7 %fusion.63 = (f32[3,1,4,256]{3,2,1,0:T(4,128)S(1)}, f32[3,1,4,256]{3,2,1,0:T(4,128)S(1)}) fusion(f32[3,16,4,256]{3,2,1,0:T(4,128)} %param.9), kind=kLoop, calls=%fused_computation.85 | loop fusion | bytes 49152 | tf_op jit(solution)/shard_map/slice | solution.py:68
  0.8 2.1 %collective-permute-start.1 = (f32[3,1,4,256]{3,1,2,0:T(1,128)S(1)}, f32[3,1,4,256]{3,1,2,0:T(1,128)S(1)}, u32[]{:S(2)}, u32[]{:S(2)}) collective-permute-start(f32[3,1,4,256]{3,1,2,0:T(1,128)S(1)} %copy.107), channel_id=1, source_target_pairs={{0,1},{1,2},{2,3},{3,4},{4,5},{5,6},{6,7},{7,0},{8,9},{9,10},{10,1... | collective-permute-start | bytes 36872 | tf_op jit(solution)/shard_map/ppermute | solution.py:65
  2.9 2.4 %collective-permute-start = (f32[3,1,4,256]{3,1,2,0:T(1,128)S(1)}, f32[3,1,4,256]{3,1,2,0:T(1,128)S(1)}, u32[]{:S(2)}, u32[]{:S(2)}) collective-permute-start(f32[3,1,4,256]{3,1,2,0:T(1,128)S(1)} %copy.105), channel_id=1, source_target_pairs={{1,0},{2,1},{3,2},{4,3},{5,4},{6,5},{7,6},{0,7},{9,8},{10,9},{11,1... | collective-permute-start | bytes 36872 | tf_op jit(solution)/shard_map/ppermute | solution.py:68
  5.2 2.2 %shard_map.91 = f32[8,2048]{1,0:T(8,128)} custom-call(f32[3,128]{1,0:T(4,128)} %pv_ref.1, f32[1,128]{1,0:T(1,128)} %bitcast.52, f32[1,128]{1,0:T(1,128)} %bitcast.53, s32[1,2048]{1,0:T(1,128)} %sp_ref.1, s32[1,128]{1,0:T(1,128)} %cnt_ref.1, f32[3,1,2048]{2,1,0:T(1,128)} %off_ref.1), custom_call_target="tpu_custom_call" | custom-call | tf_op jit(solution)/shard_map/pallas_call | solution.py:46
  7.4 1.0 %reshape.212 = f32[8,128,16]{2,1,0:T(8,128)S(1)} reshape(f32[8,2048]{1,0:T(8,128)} %shard_map.91) | data formatting | bytes 131072 | tf_op jit(solution)/shard_map/reshape | solution.py:126
  8.5 0.2 copy.97
  8.7 0.7 %copy.98 = f32[128,1,128]{2,1,0:T(1,128)} copy(f32[128,1,128]{0,2,1:T(8,128)S(1)} %bitcast.46) | data formatting | bytes 131072 | tf_op jit(solution)/shard_map/all_to_all | solution.py:128
  9.4 9.2 %all-to-all-start = ((f32[128,1,128]{2,1,0:T(1,128)}), f32[128,1,128]{2,1,0:T(1,128)S(1)}, u32[]{:S(2)}, u32[]{:S(2)}) async-start(f32[128,1,128]{2,1,0:T(1,128)} %copy.98), calls=%async_computation | async-start | bytes 131072 | tf_op jit(solution)/shard_map/all_to_all | solution.py:128
  18.7 0.1 fusion.61
  18.7 0.1 fusion.62
  18.9 0.5 copy-done.2
  19.6 8.8 %all-to-all-done = f32[128,1,128]{2,1,0:T(1,128)S(1)} async-done(((f32[128,1,128]{2,1,0:T(1,128)}), f32[128,1,128]{2,1,0:T(1,128)S(1)}, u32[]{:S(2)}, u32[]{:S(2)}) %all-to-all-start) | async-done | bytes 65568 | tf_op jit(solution)/shard_map/all_to_all | solution.py:128
  28.4 0.1 copy.99
  28.5 0.1 copy.102
  28.6 0.1 sub.119
  28.7 0.1 copy.103
  28.8 0.1 sub.126
  28.9 0.1 copy.101
  29.0 0.1 squeeze.4
  29.1 0.1 copy.100
  29.2 0.1 slice.83
  29.6 0.1 copy.104
  29.7 0.1 sub.133
  29.8 2.1 %fusion.36 = f32[3,16,4,256]{3,1,2,0:T(8,128)S(1)} fusion(f32[3,16,4,256]{3,1,2,0:T(8,128)S(1)} %copy.118, f32[3,1,4,256]{3,1,2,0:T(1,128)S(1)} %collective-permute-done.1, f32[3,1,4,256]{3,1,2,0:T(1,128)S(1)} %collective-permute-done, f32[3,16,4,1]{3,1,2,0:T(8,128)S(1)} %get-tuple-element.14, f32[3,16,4,255]{3,1,2,0:T(8,128)S(1)} %get-tuple-element.16, ...), kind=kOutput, calls=%fused_computation.39 | convolution fusion | flops 610729984 | bytes 1392640 | tf_op jit(solution)/shard_map/dot_general | solution.py:90
  31.9 0.3 copy.119
  32.1 13.5 %all_to_all.30 = f32[6,16,4,256]{3,2,0,1:T(4,128)S(1)} all-to-all(f32[6,16,4,256]{3,2,0,1:T(4,128)S(1)} %copy.119), channel_id=1, replica_groups=mesh['gx'=16,'gy'=8] {'gx'}, dimensions={1} | all-to-all | bytes 786432 | tf_op jit(solution)/shard_map/all_to_all | solution.py:143
  45.7 0.1 slice.101
  45.8 0.1 slice.99
  45.9 0.4 convolution_bitcast_fusion
  46.3 0.2 copy.122
  46.5 11.9 %all_to_all.31 = f32[3,1,64,256]{3,1,0,2:T(1,128)S(1)} all-to-all(f32[3,1,64,256]{3,1,0,2:T(1,128)S(1)} %copy.122), channel_id=1, replica_groups=mesh['gx'=16,'gy'=8] {'gx'}, dimensions={2} | all-to-all | bytes 393216 | tf_op jit(solution)/shard_map/all_to_all | solution.py:149
  58.4 0.7 %all_to_all.26 = f32[3,16,4,256]{3,2,1,0:T(4,128)} reshape(f32[3,1,64,256]{3,2,0,1:T(8,128)S(1)} %copy.123) | data formatting | bytes 393216 | tf_op jit(solution)/shard_map/all_to_all | solution.py:149
  (30 shorter events, 0.6 us)
Async XLA Ops:
  0.0 45.9 %copy-start = (f32[64,64]{1,0:T(8,128)S(1)}, f32[64,64]{1,0:T(8,128)}, u32[]{:S(2)}) copy-start(f32[64,64]{1,0:T(8,128)} %param.17) | copy-start | bytes 49156
  0.8 29.0 %collective-permute-start.1 = (f32[3,1,4,256]{3,1,2,0:T(1,128)S(1)}, f32[3,1,4,256]{3,1,2,0:T(1,128)S(1)}, u32[]{:S(2)}, u32[]{:S(2)}) collective-permute-start(f32[3,1,4,256]{3,1,2,0:T(1,128)S(1)} %copy.107), channel_id=1, source_target_pairs={{0,1},{1,2},{2,3},{3,4},{4,5},{5,6},{6,7},{7,0},{8,9},{9,10},{10,1... | collective-permute-start | bytes 36872 | tf_op jit(solution)/shard_map/ppermute | solution.py:65
  2.9 26.9 %collective-permute-start = (f32[3,1,4,256]{3,1,2,0:T(1,128)S(1)}, f32[3,1,4,256]{3,1,2,0:T(1,128)S(1)}, u32[]{:S(2)}, u32[]{:S(2)}) collective-permute-start(f32[3,1,4,256]{3,1,2,0:T(1,128)S(1)} %copy.105), channel_id=1, source_target_pairs={{1,0},{2,1},{3,2},{4,3},{5,4},{6,5},{7,6},{0,7},{9,8},{10,9},{11,1... | collective-permute-start | bytes 36872 | tf_op jit(solution)/shard_map/ppermute | solution.py:68
  8.5 10.1 %copy-start.1 = (f32[3,16,4,256]{3,2,1,0:T(4,128)S(1)}, f32[3,16,4,256]{3,2,1,0:T(4,128)}, u32[]{:S(2)}) copy-start(f32[3,16,4,256]{3,2,1,0:T(4,128)} %param.9) | copy-start | bytes 589828
  9.4 19.0 %all-to-all-start = ((f32[128,1,128]{2,1,0:T(1,128)}), f32[128,1,128]{2,1,0:T(1,128)S(1)}, u32[]{:S(2)}, u32[]{:S(2)}) async-start(f32[128,1,128]{2,1,0:T(1,128)} %copy.98), calls=%async_computation | async-start | bytes 131072 | tf_op jit(solution)/shard_map/all_to_all | solution.py:128
  18.6 0.7 %copy-start.2 = (s32[1,2048]{1,0:T(1,128)S(1)}, s32[1,2048]{1,0:T(1,128)}, u32[]{:S(2)}) copy-start(s32[1,2048]{1,0:T(1,128)} %param.16) | copy-start | bytes 24580
